TPU v7x, 256 devices: a whole 4x4x8 slice. The times are simulated.
256 devices in a mesh: dp: 16 (over y, x_hi, core), tensor: 16 (over x_lo, z).
Axes of the slice: x: 4 (x_hi: 2, x_lo: 2; x = x_hi * 2 + x_lo), y: 4, z: 8, core: 2. Of those that a mesh axis runs over, the one named last changes fastest.
Arguments:
- tokens: bfloat16 [768, 6144], P('dp', 'tensor'), may hold values from -6 to 6
- routes: int32 [768, 2], P('dp'), may hold values from 0 to 3, all different within a row; in each aligned block of 48 rows (0 to 47, 48 to 95, ...) at most 32 rows name the same one
- gate_weights: bfloat16 [768, 2], P('dp'), may hold values from 0.25 to 1
- gate_matrix: bfloat16 [16, 6144, 2048], P('dp', None, 'tensor'), may hold values from -0.078125 to 0.078125
- up_matrix: bfloat16 [16, 6144, 2048], P('dp', None, 'tensor'), may hold values from -0.078125 to 0.078125
- down_matrix: bfloat16 [16, 2048, 6144], P('dp', 'tensor'), may hold values from -0.0625 to 0.0625
- cotangent: bfloat16 [768, 6144], P('dp', 'tensor'), may hold values from -6 to 6
Outputs:
- layer_out: bfloat16 [768, 6144], P('dp', 'tensor')
- token_gradient: bfloat16 [768, 6144], P('dp', 'tensor')
- gate_gradient: bfloat16 [16, 6144, 2048], P('dp', None, 'tensor')
- up_gradient: bfloat16 [16, 6144, 2048], P('dp', None, 'tensor')
- down_gradient: bfloat16 [16, 2048, 6144], P('dp', 'tensor')
Inputs may be any that keep to these rules, and one draw needn't show every extreme that they name: `routes`: within the rows of one dp index (aligned blocks of 48 rows) no expert is named by more than 32 rows, and in some such block one expert is named by exactly 32; the two experts of a row differ.
All inputs are finite; a program needn't handle non-finite values.
Results may differ from a plain program's by a relative error of at most 0.018.
Values may be sent and summed in bfloat16 or wider, within the bound.
No kernel may reach another device: no remote copies, remote signals or barrier semaphores. Data moves between devices by JAX's collectives and lax.ppermute only.
A program may use at most 128 MiB of HBM per device.

v0:
```python
import jax
import jax.numpy as jnp
from jax import lax
from jax.sharding import PartitionSpec as P

EXPERTS = 4
CAP = 32


precise = lax.Precision.HIGHEST


def rounded(values):
    return lax.optimization_barrier(values.astype(jnp.bfloat16)).astype(jnp.float32)


def slot_tables(routes, gate_weights, capacity):
    experts = jnp.arange(EXPERTS, dtype=jnp.int32)
    hit_mask = routes[:, :, None] == experts[None, None, :]
    chosen = jnp.any(hit_mask, axis=1)
    weights = jnp.sum(
        jnp.where(hit_mask, gate_weights.astype(jnp.float32)[:, :, None], jnp.float32(0.0)), axis=1
    )
    places = jnp.cumsum(chosen.astype(jnp.int32), axis=0) - 1
    columns = jnp.arange(capacity, dtype=jnp.int32)
    onehot = (places[:, :, None] == columns[None, None, :]) & chosen[:, :, None]
    return (onehot, weights)


def per_device(tokens, routes, gate_weights, gate_matrix, up_matrix, down_matrix, cotangent):
    feature_cols = tokens.shape[1]
    expert_span = lax.axis_size("dp") // EXPERTS
    onehot, weights = slot_tables(routes, gate_weights, CAP)
    member = onehot.astype(jnp.float32)
    scaled = member * weights[:, :, None]

    def spread(slot_table):
        widened = jnp.broadcast_to(
            slot_table[:, :, None, :], (slot_table.shape[0], EXPERTS, expert_span, CAP)
        )
        return widened.reshape(slot_table.shape[0], EXPERTS * expert_span * CAP)

    member_wide = spread(member)
    scaled_wide = spread(scaled)
    token_send = jnp.einsum(
        "tr,tc->rc", member_wide.astype(jnp.bfloat16), tokens, preferred_element_type=jnp.float32
    ).astype(jnp.bfloat16)
    grad_send = jnp.einsum(
        "tr,tc->rc", scaled_wide, cotangent.astype(jnp.float32), precision=precise
    ).astype(jnp.bfloat16)
    token_recv, grad_recv = (
        lax.all_to_all(
            token_send.reshape(-1, CAP, feature_cols), "dp", split_axis=0, concat_axis=0, tiled=True
        ),
        lax.all_to_all(
            grad_send.reshape(-1, CAP, feature_cols), "dp", split_axis=0, concat_axis=0, tiled=True
        ),
    )
    gate_local = gate_matrix[0]
    up_local = up_matrix[0]
    down_local = down_matrix[0]

    def bring_back(partial_value, slot_table):
        summed = lax.psum_scatter(
            rounded(partial_value).astype(jnp.bfloat16), "tensor", scatter_dimension=1, tiled=True
        ).astype(jnp.float32)
        returned = lax.all_to_all(
            summed.reshape(-1, CAP, feature_cols).astype(jnp.bfloat16),
            "dp",
            split_axis=0,
            concat_axis=0,
            tiled=True,
        ).astype(jnp.float32)
        return jnp.dot(
            slot_table,
            returned.reshape(-1, feature_cols),
            precision=precise,
            preferred_element_type=jnp.float32,
        )

    token_rows, grad_rows = (
        lax.all_gather(token_recv, "tensor", axis=2, tiled=True),
        lax.all_gather(grad_recv, "tensor", axis=2, tiled=True),
    )
    flat_tokens = token_rows.reshape(-1, token_rows.shape[2])
    gate_pre = jnp.dot(flat_tokens, gate_local, preferred_element_type=jnp.float32)
    up_pre = jnp.dot(flat_tokens, up_local, preferred_element_type=jnp.float32)
    sigmoid_gate = jax.nn.sigmoid(gate_pre)
    activated = gate_pre * sigmoid_gate
    hidden = (activated * up_pre).astype(jnp.bfloat16)
    partial_out = jnp.dot(hidden, down_local, preferred_element_type=jnp.float32)
    layer_out = bring_back(partial_out, scaled_wide).astype(jnp.bfloat16)
    flat_grads = grad_rows.reshape(-1, grad_rows.shape[2])
    hidden_grad = jnp.einsum(
        "rd,hd->rh", flat_grads, down_local, preferred_element_type=jnp.float32
    )
    gate_grad = (
        hidden_grad * up_pre * sigmoid_gate * (1.0 + gate_pre * (1.0 - sigmoid_gate))
    ).astype(jnp.bfloat16)
    up_grad = (hidden_grad * activated).astype(jnp.bfloat16)
    token_part = jnp.einsum(
        "rh,dh->rd", gate_grad, gate_local, preferred_element_type=jnp.float32
    ) + jnp.einsum("rh,dh->rd", up_grad, up_local, preferred_element_type=jnp.float32)
    token_gradient = bring_back(token_part, member_wide).astype(jnp.bfloat16)
    gate_gradient = jnp.einsum(
        "rd,rh->dh", flat_tokens, gate_grad, preferred_element_type=jnp.float32
    ).astype(jnp.bfloat16)[None]
    up_gradient = jnp.einsum(
        "rd,rh->dh", flat_tokens, up_grad, preferred_element_type=jnp.float32
    ).astype(jnp.bfloat16)[None]
    down_gradient = jnp.einsum(
        "rh,rd->hd", hidden, flat_grads, preferred_element_type=jnp.float32
    ).astype(jnp.bfloat16)[None]
    return (layer_out, token_gradient, gate_gradient, up_gradient, down_gradient)


def solution(mesh):
    in_specs = (
        P("dp", "tensor"),
        P("dp", None),
        P("dp", None),
        P("dp", None, "tensor"),
        P("dp", None, "tensor"),
        P("dp", "tensor", None),
        P("dp", "tensor"),
    )
    out_specs = (
        P("dp", "tensor"),
        P("dp", "tensor"),
        P("dp", None, "tensor"),
        P("dp", None, "tensor"),
        P("dp", "tensor", None),
    )
    return jax.shard_map(
        per_device, mesh=mesh, in_specs=in_specs, out_specs=out_specs, check_vma=False
    )
```

profile of v0, /device:TPU:2, one launch (start us, length us, event | category | flops | bytes accessed | tf_op | source)
XLA Modules:
  0.0 408.5 jit_solution(6520651275300490506)
XLA Ops:
  10.0 17.0 %all_to_all.20 = bf16[16,32,384]{2,1,0:T(8,128)(2,1)} all-to-all(bf16[16,32,384]{2,1,0:T(8,128)(2,1)S(1)} %bitcast.68), channel_id=1, replica_groups=mesh['dp'=16,'tensor'=16] {'dp'}, dimensions={0} | all-to-all | bytes 786432 | tf_op jit(solution)/shard_map/all_to_all | solution.py:52
  28.4 1.2 convolution_convert_fusion.4
  29.6 14.2 %all_to_all.21 = bf16[16,32,384]{2,1,0:T(8,128)(2,1)} all-to-all(bf16[16,32,384]{2,1,0:T(8,128)(2,1)S(1)} %bitcast.71), channel_id=1, replica_groups=mesh['dp'=16,'tensor'=16] {'dp'}, dimensions={0} | all-to-all | bytes 786432 | tf_op jit(solution)/shard_map/all_to_all | solution.py:55
  43.9 64.8 %all-gather.3.cloned.1.call-done = bf16[16,32,6144]{2,1,0:T(8,128)(2,1)} async-done(((bf16[16,32,384]{2,1,0:T(8,128)(2,1)}), bf16[16,32,6144]{2,1,0:T(8,128)(2,1)}) %all-gather.3.cloned.1.call-update) | async-done | bytes 6291472 | tf_op jit(solution)/shard_map/all_gather | solution.py:82
  108.7 5.9 %fusion.7 = f32[512,128]{1,0:T(8,128)} fusion(bf16[512,6144]{1,0:T(8,128)(2,1)} %bitcast.58, bf16[1,6144,128]{2,1,0:T(8,128)(2,1)} %param.11), kind=kOutput, calls=%fused_computation.12 | convolution fusion | flops 805306368 | bytes 8126464 | tf_op jit(solution)/shard_map/dot_general | solution.py:87
  114.6 2.5 fusion.11
  117.1 73.5 %all-gather.5.cloned.1.call-done = bf16[16,32,6144]{2,1,0:T(8,128)(2,1)} async-done(((bf16[16,32,384]{2,1,0:T(8,128)(2,1)}), bf16[16,32,6144]{2,1,0:T(8,128)(2,1)}) %all-gather.5.cloned.1.call-update) | async-done | bytes 6291472 | tf_op jit(solution)/shard_map/all_gather | solution.py:83
  190.5 5.4 %multiply_convert_fusion = (bf16[512,128]{1,0:T(8,128)(2,1)}, bf16[512,128]{1,0:T(8,128)(2,1)}, bf16[512,128]{1,0:T(8,128)(2,1)S(1)}) fusion(f32[512,128]{1,0:T(8,128)} %fusion.11, f32[512,128]{1,0:T(8,128)} %fusion.7, bf16[512,6144]{1,0:T(8,128)(2,1)} %bitcast.64, bf16[1,128,6144]{2,1,0:T(8,128)(2,1)S(1)} %copy-done), kind=kOutput, calls=%fused_computation.22 | convolution fusion | flops 806289408 | bytes 8781824 | tf_op jit(solution)/shard_map/rd,hd->rh/dot_general | solution.py:94
  195.9 4.4 %convolution_convert_fusion = bf16[512,6144]{1,0:T(8,128)(2,1)} fusion(bf16[512,128]{1,0:T(8,128)(2,1)S(1)} %get-tuple-element.7, bf16[1,128,6144]{2,1,0:T(8,128)(2,1)S(1)} %copy-done), kind=kOutput, calls=%fused_computation.1 | convolution fusion | flops 808452096 | bytes 7995392 | tf_op jit(solution)/shard_map/dot_general | solution.py:91
  200.3 8.6 %copy.24 = bf16[512,6144]{0,1:T(8,128)(2,1)} copy(bf16[512,6144]{1,0:T(8,128)(2,1)} %convolution_convert_fusion) | data formatting | bytes 12582912
  209.2 2.8 fusion.9
  212.0 4.5 %add_convert_fusion = bf16[512,6144]{1,0:T(8,128)(2,1)} fusion(f32[512,6144]{1,0:T(8,128)S(1)} %fusion.9, bf16[512,128]{1,0:T(8,128)(2,1)S(1)} %copy-done.7, bf16[1,6144,128]{2,1,0:T(8,128)(2,1)S(1)} %copy-done.3), kind=kOutput, calls=%fused_computation | convolution fusion | flops 811597824 | bytes 20578304 | tf_op jit(solution)/shard_map/rh,dh->rd/dot_general | solution.py:103
  216.5 8.7 %copy.26 = bf16[512,6144]{0,1:T(8,128)(2,1)} copy(bf16[512,6144]{1,0:T(8,128)(2,1)} %add_convert_fusion) | data formatting | bytes 12582912
  226.2 5.9 %fusion.1 = bf16[1,6144,128]{2,1,0:T(8,128)(2,1)} fusion(bf16[512,6144]{1,0:T(8,128)(2,1)} %bitcast.59, bf16[512,128]{1,0:T(8,128)(2,1)S(1)} %copy-done.8), kind=kOutput, calls=%fused_computation.6 | convolution fusion | flops 806092800 | bytes 7995392 | tf_op jit(solution)/shard_map/rd,rh->dh/dot_general | solution.py:108
  232.1 62.3 %reduce-scatter.7.cloned.1.call-done = bf16[384,512]{1,0:T(8,128)(2,1)} async-done(((bf16[6144,512]{1,0:T(8,128)(2,1)}), bf16[384,512]{1,0:T(8,128)(2,1)}) %reduce-scatter.7.cloned.1.call-update) | async-done | bytes 393232
  294.4 1.9 copy.25
  296.3 6.1 %all-to-all-start.1 = ((bf16[16,32,384]{2,1,0:T(8,128)(2,1)}), bf16[16,32,384]{2,1,0:T(8,128)(2,1)S(1)}, u32[]{:S(2)}, u32[]{:S(2)}) async-start(bf16[16,32,384]{2,1,0:T(8,128)(2,1)} %bitcast.7), calls=%async_computation.1 | async-start | bytes 786432 | tf_op jit(solution)/shard_map/all_to_all | solution.py:67
  302.4 5.8 %fusion = bf16[1,6144,128]{2,1,0:T(8,128)(2,1)} fusion(bf16[512,6144]{1,0:T(8,128)(2,1)} %bitcast.60, bf16[512,128]{1,0:T(8,128)(2,1)S(1)} %copy-done.6), kind=kOutput, calls=%fused_computation.5 | convolution fusion | flops 806092800 | bytes 7995392 | tf_op jit(solution)/shard_map/rd,rh->dh/dot_general | solution.py:105
  308.2 73.1 %reduce-scatter.9.cloned.1.call-done = bf16[384,512]{1,0:T(8,128)(2,1)} async-done(((bf16[6144,512]{1,0:T(8,128)(2,1)}), bf16[384,512]{1,0:T(8,128)(2,1)}) %reduce-scatter.9.cloned.1.call-update) | async-done | bytes 393232
  381.3 1.9 copy.27
  383.2 6.7 %all-to-all-start.3 = ((bf16[16,32,384]{2,1,0:T(8,128)(2,1)}), bf16[16,32,384]{2,1,0:T(8,128)(2,1)S(1)}, u32[]{:S(2)}, u32[]{:S(2)}) async-start(bf16[16,32,384]{2,1,0:T(8,128)(2,1)} %bitcast.11), calls=%async_computation.3 | async-start | bytes 786432 | tf_op jit(solution)/shard_map/all_to_all | solution.py:67
  389.9 5.0 %fusion.2 = bf16[1,128,6144]{2,1,0:T(8,128)(2,1)} fusion(bf16[512,128]{1,0:T(8,128)(2,1)S(1)} %get-tuple-element.7, bf16[512,6144]{1,0:T(8,128)(2,1)} %bitcast.65), kind=kOutput, calls=%fused_computation.7 | convolution fusion | flops 806092800 | bytes 7995392 | tf_op jit(solution)/shard_map/rh,rd->hd/dot_general | solution.py:111
  395.9 5.0 %all-to-all-done.3 = bf16[16,32,384]{2,1,0:T(8,128)(2,1)S(1)} async-done(((bf16[16,32,384]{2,1,0:T(8,128)(2,1)}), bf16[16,32,384]{2,1,0:T(8,128)(2,1)S(1)}, u32[]{:S(2)}, u32[]{:S(2)}) %all-to-all-start.3) | async-done | bytes 393248 | tf_op jit(solution)/shard_map/all_to_all | solution.py:67
  400.9 1.0 convolution_convert_fusion.6
  (42 shorter events, 6.5 us)
Async XLA Ops:
  7.2 183.4 %copy-start = (bf16[1,128,6144]{2,1,0:T(8,128)(2,1)S(1)}, bf16[1,128,6144]{2,1,0:T(8,128)(2,1)}, u32[]{:S(2)}) copy-start(bf16[1,128,6144]{2,1,0:T(8,128)(2,1)} %param.12) | copy-start | bytes 4718596
  7.2 101.5 %all-gather.3.cloned.1.call-start = ((), (), s32[]{:S(2)}) async-start(), calls=%async_computation.6 | async-start | bytes 6684672 | tf_op jit(solution)/shard_map/all_gather | solution.py:82
  8.0 106.5 %copy-start.2 = (bf16[1,6144,128]{2,1,0:T(8,128)(2,1)S(1)}, bf16[1,6144,128]{2,1,0:T(8,128)(2,1)}, u32[]{:S(2)}) copy-start(bf16[1,6144,128]{2,1,0:T(8,128)(2,1)} %param.10) | copy-start | bytes 4718596
  8.3 0.6 copy-start.4
  26.9 163.6 %all-gather.5.cloned.1.call-start = ((), (), s32[]{:S(2)}) async-start(), calls=%async_computation.7 | async-start | bytes 6684672 | tf_op jit(solution)/shard_map/all_gather | solution.py:83
  43.9 250.6 %reduce-scatter.7.cloned.1.call-start = ((), (), s32[]{:S(2)}) async-start(), calls=%async_computation.8 | async-start | bytes 6684672
  108.7 5.9 %copy-start.1 = (bf16[16,32,6144]{2,1,0:T(8,128)(2,1)S(1)}, bf16[16,32,6144]{2,1,0:T(8,128)(2,1)}, u32[]{:S(2)}) copy-start(bf16[16,32,6144]{2,1,0:T(8,128)(2,1)} %all-gather.3.cloned.1.call-done) | copy-start | bytes 18874372
  208.9 172.4 %reduce-scatter.9.cloned.1.call-start = ((), (), s32[]{:S(2)}) async-start(), calls=%async_computation.9 | async-start | bytes 6684672
  209.2 2.9 copy-start.3
  209.2 2.9 copy-start.7
  225.3 0.9 copy-start.8
  226.2 76.2 %copy-start.6 = (bf16[512,128]{1,0:T(8,128)(2,1)S(1)}, bf16[512,128]{1,0:T(8,128)(2,1)}, u32[]{:S(2)}) copy-start(bf16[512,128]{1,0:T(8,128)(2,1)} %get-tuple-element.6) | copy-start | bytes 393220
  296.3 86.9 %all-to-all-start.1 = ((bf16[16,32,384]{2,1,0:T(8,128)(2,1)}), bf16[16,32,384]{2,1,0:T(8,128)(2,1)S(1)}, u32[]{:S(2)}, u32[]{:S(2)}) async-start(bf16[16,32,384]{2,1,0:T(8,128)(2,1)} %bitcast.7), calls=%async_computation.1 | async-start | bytes 786432 | tf_op jit(solution)/shard_map/all_to_all | solution.py:67
  383.2 17.6 %copy-start.5 = (f32[48,4,32]{0,2,1:T(8,128)S(1)}, f32[48,4,32]{0,2,1:T(8,128)}, u32[]{:S(2)}) copy-start(f32[48,4,32]{0,2,1:T(8,128)} %copy-done.4) | copy-start | bytes 73732
  383.2 17.6 %all-to-all-start.3 = ((bf16[16,32,384]{2,1,0:T(8,128)(2,1)}), bf16[16,32,384]{2,1,0:T(8,128)(2,1)S(1)}, u32[]{:S(2)}, u32[]{:S(2)}) async-start(bf16[16,32,384]{2,1,0:T(8,128)(2,1)} %bitcast.11), calls=%async_computation.3 | async-start | bytes 786432 | tf_op jit(solution)/shard_map/all_to_all | solution.py:67
Sparse Core Ops, SparseCore 0:
  27.1 81.5 all-gather.2
  110.5 79.9 all-gather.4
  209.1 85.3 reduce-scatter.6
  296.8 84.4 reduce-scatter.8
where the time goes:
time: 411 us; the launch traced here: 408 us
  waiting for transfers between devices  279 us (68%)
  matrix products  46.4 us (11%)
  blocking collectives  31.2 us (8%)
  local copies, waits for them, and re-layouts  22.9 us (6%)
  between operations  13.9 us (3%)
  starting transfers between devices  13.1 us (3%)
    unnamed x6, waiting for transfers between devices  135 us
    all_gather x1, waiting for transfers between devices, per_device(): lax.all_gather(grad_recv, 'tensor', axis=2, tiled=True)  73.5 us
    all_gather x1, waiting for transfers between devices, per_device(): lax.all_gather(token_recv, 'tensor', axis=2, tiled=True)  64.8 us
    unnamed x22, local copies, waits for them, and re-layouts  22.7 us
    all_to_all x1, blocking collectives, per_device(): lax.all_to_all(token_send.reshape(-1, CAP, feature_cols), 'dp', split_axi...  17 us
    all_to_all x1, blocking collectives, per_device(): lax.all_to_all(grad_send.reshape(-1, CAP, feature_cols), 'dp', split_axis...  14.2 us
    all_to_all x2, starting transfers between devices, bring_back(): lax.all_to_all(summed.reshape(-1, CAP, feature_cols).astype(jnp.bfloat16)...  12.8 us
  transfers between devices with their start and end apart: 6, of which 5 were waited for; matrix products, arithmetic and copies ran while one was open for 12% of the time, Pallas kernels for 0%

commit v1 on v0

v1 whole, which is shorter than its diff:
```python
import jax
import jax.numpy as jnp
from jax import lax
from jax.sharding import PartitionSpec as P

EXPERTS = 4
CAP = 32


precise = lax.Precision.HIGHEST


def slot_tables(routes, gate_weights, capacity):
    experts = jnp.arange(EXPERTS, dtype=jnp.int32)
    hit_mask = routes[:, :, None] == experts[None, None, :]
    chosen = jnp.any(hit_mask, axis=1)
    weights = jnp.sum(
        jnp.where(hit_mask, gate_weights.astype(jnp.float32)[:, :, None], jnp.float32(0.0)), axis=1
    )
    places = jnp.cumsum(chosen.astype(jnp.int32), axis=0) - 1
    columns = jnp.arange(capacity, dtype=jnp.int32)
    onehot = (places[:, :, None] == columns[None, None, :]) & chosen[:, :, None]
    return (onehot, weights)


def per_device(tokens, routes, gate_weights, gate_matrix, up_matrix, down_matrix, cotangent):
    feature_cols = tokens.shape[1]
    n_dp = lax.axis_size("dp")
    expert_span = n_dp // EXPERTS
    half = n_dp // 2
    core = lax.axis_index("dp") % 2
    pair = [(d, d ^ 1) for d in range(n_dp)]
    onehot, weights = slot_tables(routes, gate_weights, CAP)
    member = onehot.astype(jnp.float32)
    scaled = member * weights[:, :, None]

    def spread(slot_table):
        widened = jnp.broadcast_to(
            slot_table[:, :, None, :], (slot_table.shape[0], EXPERTS, expert_span, CAP)
        )
        return widened.reshape(slot_table.shape[0], EXPERTS * expert_span * CAP)

    member_wide = spread(member)
    scaled_wide = spread(scaled)
    token_send = jnp.einsum(
        "tr,tc->rc", member_wide.astype(jnp.bfloat16), tokens, preferred_element_type=jnp.float32
    ).astype(jnp.bfloat16)
    grad_send = jnp.einsum(
        "tr,tc->rc", scaled_wide, cotangent.astype(jnp.float32), precision=precise
    ).astype(jnp.bfloat16)
    send = jnp.concatenate(
        [token_send.reshape(n_dp, CAP, feature_cols), grad_send.reshape(n_dp, CAP, feature_cols)],
        axis=1,
    )
    recv = lax.all_to_all(send, "dp", split_axis=0, concat_axis=0, tiled=True)
    mine = lax.dynamic_slice_in_dim(recv, core * half, half, axis=0)
    mine = mine.reshape(half, 2, CAP, feature_cols).transpose(1, 0, 2, 3)
    mine = mine.reshape(2, half * CAP, feature_cols)
    mine_full = lax.all_gather(mine, "tensor", axis=2, tiled=True)
    other_full = lax.ppermute(mine_full, "dp", pair)

    gate_local = gate_matrix[0]
    up_local = up_matrix[0]
    down_local = down_matrix[0]

    def forward(rows):
        gate_pre = jnp.dot(rows, gate_local, preferred_element_type=jnp.float32)
        up_pre = jnp.dot(rows, up_local, preferred_element_type=jnp.float32)
        sigmoid_gate = jax.nn.sigmoid(gate_pre)
        activated = gate_pre * sigmoid_gate
        hidden = (activated * up_pre).astype(jnp.bfloat16)
        out_t = jnp.einsum(
            "hd,rh->dr", down_local, hidden, preferred_element_type=jnp.float32
        ).astype(jnp.bfloat16)
        return gate_pre, up_pre, sigmoid_gate, activated, hidden, out_t

    def backward(rows, grads, gate_pre, up_pre, sigmoid_gate, activated):
        hidden_grad = jnp.einsum(
            "rd,hd->rh", grads, down_local, preferred_element_type=jnp.float32
        )
        gate_grad = (
            hidden_grad * up_pre * sigmoid_gate * (1.0 + gate_pre * (1.0 - sigmoid_gate))
        ).astype(jnp.bfloat16)
        up_grad = (hidden_grad * activated).astype(jnp.bfloat16)
        back_t = (
            jnp.einsum("dh,rh->dr", gate_local, gate_grad, preferred_element_type=jnp.float32)
            + jnp.einsum("dh,rh->dr", up_local, up_grad, preferred_element_type=jnp.float32)
        ).astype(jnp.bfloat16)
        return gate_grad, up_grad, back_t

    rows_a, grads_a = mine_full[0], mine_full[1]
    rows_b, grads_b = other_full[0], other_full[1]
    fa = forward(rows_a)
    fb = forward(rows_b)

    def combine(own_t, partner_t):
        summed = own_t.astype(jnp.float32) + partner_t.astype(jnp.float32)
        scattered = lax.psum_scatter(
            summed.astype(jnp.bfloat16), "tensor", scatter_dimension=0, tiled=True
        )
        return scattered.T

    out_partner = lax.ppermute(fb[5], "dp", pair)
    out_rows = combine(fa[5], out_partner)

    ga, ua, back_a = backward(rows_a, grads_a, *fa[:4])
    gb, ub, back_b = backward(rows_b, grads_b, *fb[:4])
    back_partner = lax.ppermute(back_b, "dp", pair)
    back_rows = combine(back_a, back_partner)

    gate_gradient = (
        jnp.einsum("rd,rh->dh", rows_a, ga, preferred_element_type=jnp.float32)
        + jnp.einsum("rd,rh->dh", rows_b, gb, preferred_element_type=jnp.float32)
    ).astype(jnp.bfloat16)[None]
    up_gradient = (
        jnp.einsum("rd,rh->dh", rows_a, ua, preferred_element_type=jnp.float32)
        + jnp.einsum("rd,rh->dh", rows_b, ub, preferred_element_type=jnp.float32)
    ).astype(jnp.bfloat16)[None]
    down_gradient = (
        jnp.einsum("rh,rd->hd", fa[4], grads_a, preferred_element_type=jnp.float32)
        + jnp.einsum("rh,rd->hd", fb[4], grads_b, preferred_element_type=jnp.float32)
    ).astype(jnp.bfloat16)[None]

    done = jnp.concatenate(
        [
            out_rows.reshape(half, CAP, feature_cols),
            back_rows.reshape(half, CAP, feature_cols),
        ],
        axis=1,
    )
    ret_send = lax.dynamic_update_slice_in_dim(
        jnp.zeros((n_dp, 2 * CAP, feature_cols), jnp.bfloat16), done, core * half, axis=0
    )
    returned = lax.all_to_all(ret_send, "dp", split_axis=0, concat_axis=0, tiled=True).astype(
        jnp.float32
    )
    returned_out = returned[:, :CAP].reshape(-1, feature_cols)
    returned_back = returned[:, CAP:].reshape(-1, feature_cols)
    layer_out = jnp.dot(
        scaled_wide, returned_out, precision=precise, preferred_element_type=jnp.float32
    ).astype(jnp.bfloat16)
    token_gradient = jnp.dot(
        member_wide, returned_back, precision=precise, preferred_element_type=jnp.float32
    ).astype(jnp.bfloat16)
    return (layer_out, token_gradient, gate_gradient, up_gradient, down_gradient)


def solution(mesh):
    in_specs = (
        P("dp", "tensor"),
        P("dp", None),
        P("dp", None),
        P("dp", None, "tensor"),
        P("dp", None, "tensor"),
        P("dp", "tensor", None),
        P("dp", "tensor"),
    )
    out_specs = (
        P("dp", "tensor"),
        P("dp", "tensor"),
        P("dp", None, "tensor"),
        P("dp", None, "tensor"),
        P("dp", "tensor", None),
    )
    return jax.shard_map(
        per_device, mesh=mesh, in_specs=in_specs, out_specs=out_specs, check_vma=False
    )
```

time: 411 us -> 335 us (0.82)
  waiting for transfers between devices: 279 us -> 240 us
  blocking collectives: 31.2 us -> 0 us
  local copies, waits for them, and re-layouts: 22.9 us -> 16.9 us
    all_gather x2 -> x1, waiting for transfers between devices: 138 us -> 81.2 us  [per_device(): mine_full = lax.all_gather(mine, 'tensor', axis=2, tiled=True)]
    all_to_all x2 -> x0, blocking collectives: 31.2 us -> none  [the longest x1 17 us: per_device(): lax.all_to_all(token_send.reshape(-1, CAP, feature_cols), 'dp', split_axi...]
    all_to_all x2, waiting for transfers between devices: 4.95 us -> 21.3 us  [the longest x1 15.2 us: per_device(): recv = lax.all_to_all(send, 'dp', split_axis=0, concat_axis=0, tiled=True)]
    ppermute x0 -> x3, waiting for transfers between devices: none -> 16.1 us  [the longest x1 10.4 us: per_device(): other_full = lax.ppermute(mine_full, 'dp', pair)]
    unnamed x6 -> x5, waiting for transfers between devices: 135 us -> 122 us
    unnamed x22 -> x40, local copies, waits for them, and re-layouts: 22.7 us -> 13.8 us
    dot_general x11 -> x20, matrix products: 44.2 us -> 42 us  [the longest x1 4.83 us: per_device(): jnp.einsum('rd,rh->dh', rows_a, ga, preferred_element_type=jnp.float32)]
  transfers between devices with their start and end apart: 6 -> 8, of which waited for: 5 -> 8; matrix products, arithmetic and copies ran while one was open for 12% -> 11% of each run, Pallas kernels for 0% -> 0%
where the time goes in v1:
time: 335 us; the launch traced here: 333 us
  waiting for transfers between devices  240 us (72%)
  matrix products  44.4 us (13%)
  local copies, waits for them, and re-layouts  16.9 us (5%)
  between operations  14 us (4%)
  starting transfers between devices  13.2 us (4%)
  other arithmetic  4.1 us (1%)
    unnamed x5, waiting for transfers between devices  122 us
    all_gather x1, waiting for transfers between devices, per_device(): mine_full = lax.all_gather(mine, 'tensor', axis=2, tiled=True)  81.2 us
    all_to_all x1, waiting for transfers between devices, per_device(): recv = lax.all_to_all(send, 'dp', split_axis=0, concat_axis=0, tiled=True)  15.2 us
    unnamed x40, local copies, waits for them, and re-layouts  13.8 us
    ppermute x1, waiting for transfers between devices, per_device(): other_full = lax.ppermute(mine_full, 'dp', pair)  10.4 us
  transfers between devices with their start and end apart: 8, of which 8 were waited for; matrix products, arithmetic and copies ran while one was open for 11% of the time, Pallas kernels for 0%

profile of v1, /device:TPU:2, one launch (start us, length us, event | category | flops | bytes accessed | tf_op | source)
XLA Modules:
  0.0 333.0 jit_solution(3814287716433278154)
XLA Ops:
  9.7 1.3 convolution_convert_fusion.2
  13.1 6.2 %all-to-all-start = ((bf16[16,64,384]{2,1,0:T(8,128)(2,1)}), bf16[16,64,384]{2,1,0:T(8,128)(2,1)}, u32[]{:S(2)}, u32[]{:S(2)}) async-start(bf16[16,64,384]{2,1,0:T(8,128)(2,1)} %pad_maximum_fusion), calls=%async_computation | async-start | bytes 1572864 | tf_op jit(solution)/shard_map/all_to_all | solution.py:55
  19.3 15.2 %all-to-all-done = bf16[16,64,384]{2,1,0:T(8,128)(2,1)} async-done(((bf16[16,64,384]{2,1,0:T(8,128)(2,1)}), bf16[16,64,384]{2,1,0:T(8,128)(2,1)}, u32[]{:S(2)}, u32[]{:S(2)}) %all-to-all-start) | async-done | bytes 786464 | tf_op jit(solution)/shard_map/all_to_all | solution.py:55
  36.4 81.2 %all-gather.2.cloned.1.call-done = bf16[2,256,6144]{2,1,0:T(8,128)(2,1)} async-done(((bf16[2,256,384]{2,1,0:T(8,128)(2,1)}), bf16[2,256,6144]{2,1,0:T(8,128)(2,1)}) %all-gather.2.cloned.1.call-update) | async-done | bytes 6291472 | tf_op jit(solution)/shard_map/all_gather | solution.py:59
  117.6 10.4 %collective-permute-done = bf16[2,256,6144]{2,1,0:T(8,128)(2,1)S(1)} collective-permute-done((bf16[2,256,6144]{2,1,0:T(8,128)(2,1)}, bf16[2,256,6144]{2,1,0:T(8,128)(2,1)S(1)}, u32[]{:S(2)}, u32[]{:S(2)}) %collective-permute-start) | collective-permute-done | bytes 6291488 | tf_op jit(solution)/shard_map/ppermute | solution.py:60
  130.7 1.6 multiply_convert_fusion.4
  137.4 1.6 multiply_convert_fusion.5
  140.2 2.7 add_convert_fusion
  143.0 4.7 %copy.33 = bf16[6144,256]{1,0:T(8,128)(2,1)} copy(bf16[6144,256]{0,1:T(8,128)(2,1)} %add_convert_fusion) | data formatting | bytes 6291456
  149.8 5.5 %collective-permute-done.1 = bf16[6144,256]{0,1:T(8,128)(2,1)S(1)} collective-permute-done((bf16[6144,256]{0,1:T(8,128)(2,1)S(1)}, bf16[6144,256]{0,1:T(8,128)(2,1)S(1)}, u32[]{:S(2)}, u32[]{:S(2)}) %collective-permute-start.1) | collective-permute-done | bytes 3145760 | tf_op jit(solution)/shard_map/ppermute | solution.py:103
  155.3 2.6 add_convert_fusion.1
  157.9 4.8 %copy.31 = bf16[6144,256]{1,0:T(8,128)(2,1)} copy(bf16[6144,256]{0,1:T(8,128)(2,1)} %add_convert_fusion.1) | data formatting | bytes 6291456
  162.7 4.2 %fusion.14 = f32[128,6144]{1,0:T(8,128)} fusion(bf16[256,128]{1,0:T(8,128)(2,1)S(1)} %copy-done.13, bf16[2,256,6144]{2,1,0:T(8,128)(2,1)} %all-gather.2.cloned.1.call-done), kind=kOutput, calls=%fused_computation.27 | convolution fusion | flops 402653184 | bytes 6356992 | tf_op jit(solution)/shard_map/rh,rd->hd/dot_general | solution.py:120
  167.0 3.1 fusion.17
  170.1 4.8 %fusion.18 = f32[6144,128]{1,0:T(8,128)} fusion(bf16[256,128]{1,0:T(8,128)(2,1)S(1)} %copy-done.10, bf16[2,256,6144]{2,1,0:T(8,128)(2,1)} %all-gather.2.cloned.1.call-done), kind=kOutput, calls=%fused_computation.31 | convolution fusion | flops 402653184 | bytes 6356992 | tf_op jit(solution)/shard_map/rd,rh->dh/dot_general | solution.py:112
  174.9 2.2 fusion.12
  177.1 46.1 %reduce-scatter.9.cloned.1.call-done = bf16[384,256]{1,0:T(8,128)(2,1)} async-done(((bf16[6144,256]{1,0:T(8,128)(2,1)}), bf16[384,256]{1,0:T(8,128)(2,1)}) %reduce-scatter.9.cloned.1.call-update) | async-done | bytes 196624
  223.2 1.1 copy.34
  224.3 75.6 %reduce-scatter.7.cloned.1.call-done = bf16[384,256]{1,0:T(8,128)(2,1)} async-done(((bf16[6144,256]{1,0:T(8,128)(2,1)}), bf16[384,256]{1,0:T(8,128)(2,1)}) %reduce-scatter.7.cloned.1.call-update) | async-done | bytes 196624
  299.9 1.1 copy.32
  302.8 6.3 %all-to-all-start.1 = ((bf16[16,64,384]{2,1,0:T(8,128)(2,1)}), bf16[16,64,384]{2,1,0:T(8,128)(2,1)S(1)}, u32[]{:S(2)}, u32[]{:S(2)}) async-start(bf16[16,64,384]{2,1,0:T(8,128)(2,1)} %maximum_dynamic-update-slice_fusion), calls=%async_computation.1 | async-start | bytes 1572864 | tf_op jit(solution)/shard_map/all_to_all | solution.py:134
  309.1 4.7 %fusion.11 = bf16[1,128,6144]{2,1,0:T(8,128)(2,1)} fusion(f32[128,6144]{1,0:T(8,128)} %fusion.14, bf16[256,128]{1,0:T(8,128)(2,1)S(1)} %copy-done.6, bf16[2,256,6144]{2,1,0:T(8,128)(2,1)} %copy-done.3), kind=kOutput, calls=%fused_computation.18 | convolution fusion | flops 404226048 | bytes 7929856 | tf_op jit(solution)/shard_map/rh,rd->hd/dot_general | solution.py:121
  313.9 4.3 %fusion.13 = bf16[1,6144,128]{2,1,0:T(8,128)(2,1)} fusion(f32[6144,128]{1,0:T(8,128)S(1)} %copy-done.2, bf16[256,128]{1,0:T(8,128)(2,1)S(1)} %get-tuple-element.11, bf16[2,256,6144]{2,1,0:T(8,128)(2,1)} %copy-done.3), kind=kOutput, calls=%fused_computation.20 | convolution fusion | flops 404226048 | bytes 7929856 | tf_op jit(solution)/shard_map/rd,rh->dh/dot_general | solution.py:113
  318.1 6.2 %all-to-all-done.1 = bf16[16,64,384]{2,1,0:T(8,128)(2,1)S(1)} async-done(((bf16[16,64,384]{2,1,0:T(8,128)(2,1)}), bf16[16,64,384]{2,1,0:T(8,128)(2,1)S(1)}, u32[]{:S(2)}, u32[]{:S(2)}) %all-to-all-start.1) | async-done | bytes 786464 | tf_op jit(solution)/shard_map/all_to_all | solution.py:134
  (78 shorter events, 21.3 us)
Async XLA Ops:
  7.2 123.5 %copy-start = (bf16[1,6144,128]{2,1,0:T(8,128)(2,1)S(1)}, bf16[1,6144,128]{2,1,0:T(8,128)(2,1)}, u32[]{:S(2)}) copy-start(bf16[1,6144,128]{2,1,0:T(8,128)(2,1)} %param.11) | copy-start | bytes 4718596
  9.7 118.3 %copy-start.4 = (bf16[1,128,6144]{2,1,0:T(8,128)(2,1)S(1)}, bf16[1,128,6144]{2,1,0:T(8,128)(2,1)}, u32[]{:S(2)}) copy-start(bf16[1,128,6144]{2,1,0:T(8,128)(2,1)} %param.12) | copy-start | bytes 4718596
  13.1 21.4 %all-to-all-start = ((bf16[16,64,384]{2,1,0:T(8,128)(2,1)}), bf16[16,64,384]{2,1,0:T(8,128)(2,1)}, u32[]{:S(2)}, u32[]{:S(2)}) async-start(bf16[16,64,384]{2,1,0:T(8,128)(2,1)} %pad_maximum_fusion), calls=%async_computation | async-start | bytes 1572864 | tf_op jit(solution)/shard_map/all_to_all | solution.py:55
  19.3 98.4 %all-gather.2.cloned.1.call-start = ((), (), s32[]{:S(2)}) async-start(), calls=%async_computation.4 | async-start | bytes 6684672 | tf_op jit(solution)/shard_map/all_gather | solution.py:59
  36.4 186.9 %reduce-scatter.9.cloned.1.call-start = ((), (), s32[]{:S(2)}) async-start(), calls=%async_computation.6 | async-start | bytes 3342336
  117.6 11.4 %copy-start.5 = (bf16[1,6144,128]{2,1,0:T(8,128)(2,1)S(1)}, bf16[1,6144,128]{2,1,0:T(8,128)(2,1)}, u32[]{:S(2)}) copy-start(bf16[1,6144,128]{2,1,0:T(8,128)(2,1)} %param.10) | copy-start | bytes 4718596
  117.6 10.4 %collective-permute-start = (bf16[2,256,6144]{2,1,0:T(8,128)(2,1)}, bf16[2,256,6144]{2,1,0:T(8,128)(2,1)S(1)}, u32[]{:S(2)}, u32[]{:S(2)}) collective-permute-start(bf16[2,256,6144]{2,1,0:T(8,128)(2,1)} %all-gather.2.cloned.1.call-done), channel_id=1, source_target_pairs={{0,16},{16,0},{32,48},{48,32},{64,80},{80,64},{96,112},{112,96},{1... | collective-permute-start | bytes 18874376 | tf_op jit(solution)/shard_map/ppermute | solution.py:60
  128.0 2.7 copy-start.3
  132.3 2.4 slice-start.2
  133.3 2.1 slice-start.3
  134.3 5.9 %collective-permute-start.2 = (bf16[6144,256]{0,1:T(8,128)(2,1)S(1)}, bf16[6144,256]{0,1:T(8,128)(2,1)S(1)}, u32[]{:S(2)}, u32[]{:S(2)}) collective-permute-start(bf16[6144,256]{0,1:T(8,128)(2,1)S(1)} %fusion.7), channel_id=1, source_target_pairs={{0,16},{16,0},{32,48},{48,32},{64,80},{80,64},{96,112},{112,96},{1... | collective-permute-start | bytes 9437192 | tf_op jit(solution)/shard_map/ppermute | solution.py:108
  139.1 1.0 copy-start.9
  139.1 1.2 copy-start.11
  147.8 7.5 %copy-start.13 = (bf16[256,128]{1,0:T(8,128)(2,1)S(1)}, bf16[256,128]{1,0:T(8,128)(2,1)}, u32[]{:S(2)}) copy-start(bf16[256,128]{1,0:T(8,128)(2,1)} %get-tuple-element.7) | copy-start | bytes 196612
  147.8 152.1 %reduce-scatter.7.cloned.1.call-start = ((), (), s32[]{:S(2)}) async-start(), calls=%async_computation.5 | async-start | bytes 3342336
  149.5 5.7 %collective-permute-start.1 = (bf16[6144,256]{0,1:T(8,128)(2,1)S(1)}, bf16[6144,256]{0,1:T(8,128)(2,1)S(1)}, u32[]{:S(2)}, u32[]{:S(2)}) collective-permute-start(bf16[6144,256]{0,1:T(8,128)(2,1)S(1)} %fusion.6), channel_id=1, source_target_pairs={{0,16},{16,0},{32,48},{48,32},{64,80},{80,64},{96,112},{112,96},{1... | collective-permute-start | bytes 9437192 | tf_op jit(solution)/shard_map/ppermute | solution.py:103
  162.7 4.2 %copy-start.12 = (bf16[256,128]{1,0:T(8,128)(2,1)S(1)}, bf16[256,128]{1,0:T(8,128)(2,1)}, u32[]{:S(2)}) copy-start(bf16[256,128]{1,0:T(8,128)(2,1)} %copy-done.11) | copy-start | bytes 196612
  166.9 3.1 copy-start.10
  167.0 8.0 %slice-start = ((s8[6291456]{0:T(1024)(128)(4,1)}), s8[4194304]{0:T(1024)(128)(4,1)S(1)}, s32[]{:S(2)}) async-start(s8[6291456]{0:T(1024)(128)(4,1)} %bitcast.116), calls=%async_computation.7 | async-start | bytes 8388608
  170.1 4.9 %slice-start.1 = ((s8[6291456]{0:T(1024)(128)(4,1)}), s8[2097152]{0:T(1024)(128)(4,1)S(1)}, s32[]{:S(2)}) async-start(s8[6291456]{0:T(1024)(128)(4,1)} %bitcast.116), calls=%async_computation.8 | async-start | bytes 4194304
  170.1 4.8 %copy-start.8 = (bf16[256,128]{1,0:T(8,128)(2,1)S(1)}, bf16[256,128]{1,0:T(8,128)(2,1)}, u32[]{:S(2)}) copy-start(bf16[256,128]{1,0:T(8,128)(2,1)} %copy-done.7) | copy-start | bytes 196612
  302.8 21.5 %all-to-all-start.1 = ((bf16[16,64,384]{2,1,0:T(8,128)(2,1)}), bf16[16,64,384]{2,1,0:T(8,128)(2,1)S(1)}, u32[]{:S(2)}, u32[]{:S(2)}) async-start(bf16[16,64,384]{2,1,0:T(8,128)(2,1)} %maximum_dynamic-update-slice_fusion), calls=%async_computation.1 | async-start | bytes 1572864 | tf_op jit(solution)/shard_map/all_to_all | solution.py:134
  309.1 4.8 %copy-start.2 = (f32[6144,128]{1,0:T(8,128)S(1)}, f32[6144,128]{1,0:T(8,128)}, u32[]{:S(2)}) copy-start(f32[6144,128]{1,0:T(8,128)} %fusion.18) | copy-start | bytes 9437188
  313.9 12.6 %copy-start.1 = (bf16[1,6144,128]{2,1,0:T(8,128)(2,1)S(1)}, bf16[1,6144,128]{2,1,0:T(8,128)(2,1)}, u32[]{:S(2)}) copy-start(bf16[1,6144,128]{2,1,0:T(8,128)(2,1)} %param.11) | copy-start | bytes 4718596
  (2 other events, 1.8 us)
Sparse Core Ops, SparseCore 0:
  36.5 81.1 all-gather.1
  147.9 75.3 reduce-scatter.8
  225.8 74.0 reduce-scatter.6

commit v2 on v1

--- a/solution.py
+++ b/solution.py
@@ -93,20 +93,16 @@
     fa = forward(rows_a)
     fb = forward(rows_b)
 
-    def combine(own_t, partner_t):
-        summed = own_t.astype(jnp.float32) + partner_t.astype(jnp.float32)
-        scattered = lax.psum_scatter(
-            summed.astype(jnp.bfloat16), "tensor", scatter_dimension=0, tiled=True
-        )
-        return scattered.T
-
-    out_partner = lax.ppermute(fb[5], "dp", pair)
-    out_rows = combine(fa[5], out_partner)
-
     ga, ua, back_a = backward(rows_a, grads_a, *fa[:4])
     gb, ub, back_b = backward(rows_b, grads_b, *fb[:4])
-    back_partner = lax.ppermute(back_b, "dp", pair)
-    back_rows = combine(back_a, back_partner)
+    partner = lax.ppermute(jnp.stack([fb[5], back_b]), "dp", pair)
+    own = jnp.stack([fa[5], back_a], axis=1)
+    summed = own.astype(jnp.float32) + partner.transpose(1, 0, 2).astype(jnp.float32)
+    summed = summed.astype(jnp.bfloat16).reshape(own.shape[0], -1)
+    scattered = lax.psum_scatter(summed, "tensor", scatter_dimension=0, tiled=True)
+    scattered = scattered.reshape(scattered.shape[0], 2, -1)
+    out_rows = scattered[:, 0].T
+    back_rows = scattered[:, 1].T
 
     gate_gradient = (
         jnp.einsum("rd,rh->dh", rows_a, ga, preferred_element_type=jnp.float32)

time: 335 us -> 282 us (0.84)
  waiting for transfers between devices: 240 us -> 187 us
  other arithmetic: 4.1 us -> 11.7 us
  matrix products: 44.4 us -> 39.6 us
    unnamed x5 -> x3, waiting for transfers between devices: 122 us -> 70 us
    convert_element_type x0 -> x1, other arithmetic: none -> 4.5 us  [per_device(): summed = summed.astype(jnp.bfloat16).reshape(own.shape[0], -1)]
    unnamed x40 -> x42, local copies, waits for them, and re-layouts: 13.8 us -> 11.3 us
  transfers between devices with their start and end apart: 8 -> 6, of which waited for: 8 -> 6; matrix products, arithmetic and copies ran while one was open for 11% -> 10% of each run, Pallas kernels for 0% -> 0%
where the time goes in v2:
time: 282 us; the launch traced here: 280 us
  waiting for transfers between devices  187 us (66%)
  matrix products  39.6 us (14%)
  local copies, waits for them, and re-layouts  14.5 us (5%)
  between operations  14.4 us (5%)
  starting transfers between devices  12.7 us (5%)
  other arithmetic  11.7 us (4%)
    all_gather x1, waiting for transfers between devices, per_device(): mine_full = lax.all_gather(mine, 'tensor', axis=2, tiled=True)  81.2 us
    unnamed x3, waiting for transfers between devices  70 us
    all_to_all x1, waiting for transfers between devices, per_device(): recv = lax.all_to_all(send, 'dp', split_axis=0, concat_axis=0, tiled=True)  15.2 us
    unnamed x42, local copies, waits for them, and re-layouts  11.3 us
    ppermute x1, waiting for transfers between devices, per_device(): other_full = lax.ppermute(mine_full, 'dp', pair)  10.4 us
    all_to_all x1, starting transfers between devices, per_device(): lax.all_to_all(ret_send, 'dp', split_axis=0, concat_axis=0, tiled=True)  6.31 us
    all_to_all x1, starting transfers between devices, per_device(): recv = lax.all_to_all(send, 'dp', split_axis=0, concat_axis=0, tiled=True)  6.17 us
    all_to_all x1, waiting for transfers between devices, per_device(): lax.all_to_all(ret_send, 'dp', split_axis=0, concat_axis=0, tiled=True)  6.15 us
  transfers between devices with their start and end apart: 6, of which 6 were waited for; matrix products, arithmetic and copies ran while one was open for 10% of the time, Pallas kernels for 0%

profile of v2, /device:TPU:2, one launch (start us, length us, event | category | flops | bytes accessed | tf_op | source)
XLA Modules:
  0.0 280.0 jit_solution(15985227717356916)
XLA Ops:
  10.7 1.3 convolution_convert_fusion.2
  13.1 6.2 %all-to-all-start = ((bf16[16,64,384]{2,1,0:T(8,128)(2,1)}), bf16[16,64,384]{2,1,0:T(8,128)(2,1)}, u32[]{:S(2)}, u32[]{:S(2)}) async-start(bf16[16,64,384]{2,1,0:T(8,128)(2,1)} %pad_maximum_fusion.1), calls=%async_computation | async-start | bytes 1572864 | tf_op jit(solution)/shard_map/all_to_all | solution.py:55
  19.3 15.2 %all-to-all-done = bf16[16,64,384]{2,1,0:T(8,128)(2,1)} async-done(((bf16[16,64,384]{2,1,0:T(8,128)(2,1)}), bf16[16,64,384]{2,1,0:T(8,128)(2,1)}, u32[]{:S(2)}, u32[]{:S(2)}) %all-to-all-start) | async-done | bytes 786464 | tf_op jit(solution)/shard_map/all_to_all | solution.py:55
  34.5 1.0 constant_dynamic-slice_fusion
  36.4 81.2 %all-gather.2.cloned.1.call-done = bf16[2,256,6144]{2,1,0:T(8,128)(2,1)} async-done(((bf16[2,256,384]{2,1,0:T(8,128)(2,1)}), bf16[2,256,6144]{2,1,0:T(8,128)(2,1)}) %all-gather.2.cloned.1.call-update) | async-done | bytes 6291472 | tf_op jit(solution)/shard_map/all_gather | solution.py:59
  117.6 10.4 %collective-permute-done = bf16[2,256,6144]{2,1,0:T(8,128)(2,1)S(1)} collective-permute-done((bf16[2,256,6144]{2,1,0:T(8,128)(2,1)}, bf16[2,256,6144]{2,1,0:T(8,128)(2,1)S(1)}, u32[]{:S(2)}, u32[]{:S(2)}) %collective-permute-start) | collective-permute-done | bytes 6291488 | tf_op jit(solution)/shard_map/ppermute | solution.py:60
  133.7 1.0 fusion.5
  134.7 3.1 %pad_maximum_fusion = bf16[2,6144,256]{1,2,0:T(8,128)(2,1)} fusion(bf16[1,6144,256]{1,2,0:T(8,128)(2,1)S(1)} %fusion.5, bf16[1,6144,256]{1,2,0:T(8,128)(2,1)S(1)} %fusion.4), kind=kLoop, calls=%fused_computation.21 | loop fusion | flops 3145728 | bytes 12582912 | tf_op jit(solution)/shard_map/stack | solution.py:98
  143.0 1.0 fusion.6
  144.1 4.2 %collective-permute-done.1 = bf16[2,6144,256]{1,2,0:T(8,128)(2,1)S(1)} collective-permute-done((bf16[2,6144,256]{1,2,0:T(8,128)(2,1)}, bf16[2,6144,256]{1,2,0:T(8,128)(2,1)S(1)}, u32[]{:S(2)}, u32[]{:S(2)}) %collective-permute-start.1) | collective-permute-done | bytes 6291488 | tf_op jit(solution)/shard_map/ppermute | solution.py:98
  148.2 4.5 %fusion = bf16[6144,2,256]{0,2,1:T(8,128)(2,1)} fusion(bf16[2,6144,256]{1,2,0:T(8,128)(2,1)S(1)} %collective-permute-done.1, bf16[6144,1,256]{0,2,1:T(8,128)(2,1)S(1)} %fusion.6, bf16[6144,1,256]{0,2,1:T(8,128)(2,1)S(1)} %fusion.3), kind=kLoop, calls=%fused_computation.1 | loop fusion | flops 15728640 | bytes 18874368 | tf_op jit(solution)/shard_map/convert_element_type | solution.py:101
  152.7 8.5 %copy.31 = bf16[6144,512]{1,0:T(8,128)(2,1)} copy(bf16[6144,512]{0,1:T(8,128)(2,1)} %bitcast.129) | data formatting | bytes 12582912
  162.1 4.3 %fusion.13 = f32[128,6144]{1,0:T(8,128)} fusion(bf16[256,128]{1,0:T(8,128)(2,1)S(1)} %copy-done.15, bf16[2,256,6144]{2,1,0:T(8,128)(2,1)} %all-gather.2.cloned.1.call-done), kind=kOutput, calls=%fused_computation.26 | convolution fusion | flops 402653184 | bytes 6356992 | tf_op jit(solution)/shard_map/rh,rd->hd/dot_general | solution.py:116
  166.4 4.8 %fusion.17 = f32[6144,128]{1,0:T(8,128)} fusion(bf16[256,128]{1,0:T(8,128)(2,1)S(1)} %copy-done.13, bf16[2,256,6144]{2,1,0:T(8,128)(2,1)} %all-gather.2.cloned.1.call-done), kind=kOutput, calls=%fused_computation.30 | convolution fusion | flops 402653184 | bytes 6356992 | tf_op jit(solution)/shard_map/rd,rh->dh/dot_general | solution.py:108
  171.2 3.1 %fusion.16 = f32[6144,128]{1,0:T(8,128)S(1)} fusion(bf16[256,128]{1,0:T(8,128)(2,1)S(1)} %copy-done.11, bf16[2,256,6144]{2,1,0:T(8,128)(2,1)} %all-gather.2.cloned.1.call-done), kind=kOutput, calls=%fused_computation.29 | convolution fusion | flops 402653184 | bytes 6356992 | tf_op jit(solution)/shard_map/rd,rh->dh/dot_general | solution.py:112
  174.3 2.2 fusion.11
  176.5 70.0 %reduce-scatter.4.cloned.1.call-done = bf16[384,512]{1,0:T(8,128)(2,1)} async-done(((bf16[6144,512]{1,0:T(8,128)(2,1)}), bf16[384,512]{1,0:T(8,128)(2,1)}) %reduce-scatter.4.cloned.1.call-update) | async-done | bytes 393232
  246.5 1.2 copy.32
  249.5 6.3 %all-to-all-start.1 = ((bf16[16,64,384]{2,1,0:T(8,128)(2,1)}), bf16[16,64,384]{2,1,0:T(8,128)(2,1)S(1)}, u32[]{:S(2)}, u32[]{:S(2)}) async-start(bf16[16,64,384]{2,1,0:T(8,128)(2,1)} %maximum_dynamic-update-slice_fusion), calls=%async_computation.1 | async-start | bytes 1572864 | tf_op jit(solution)/shard_map/all_to_all | solution.py:130
  255.9 4.7 %fusion.10 = bf16[1,128,6144]{2,1,0:T(8,128)(2,1)} fusion(f32[128,6144]{1,0:T(8,128)} %fusion.13, bf16[256,128]{1,0:T(8,128)(2,1)S(1)} %copy-done.7, bf16[2,256,6144]{2,1,0:T(8,128)(2,1)} %copy-done.3), kind=kOutput, calls=%fused_computation.18 | convolution fusion | flops 404226048 | bytes 7929856 | tf_op jit(solution)/shard_map/rh,rd->hd/dot_general | solution.py:117
  260.6 4.3 %fusion.12 = bf16[1,6144,128]{2,1,0:T(8,128)(2,1)} fusion(f32[6144,128]{1,0:T(8,128)S(1)} %copy-done.2, bf16[256,128]{1,0:T(8,128)(2,1)S(1)} %get-tuple-element.13, bf16[2,256,6144]{2,1,0:T(8,128)(2,1)} %copy-done.3), kind=kOutput, calls=%fused_computation.20 | convolution fusion | flops 404226048 | bytes 7929856 | tf_op jit(solution)/shard_map/rd,rh->dh/dot_general | solution.py:109
  264.9 6.1 %all-to-all-done.1 = bf16[16,64,384]{2,1,0:T(8,128)(2,1)S(1)} async-done(((bf16[16,64,384]{2,1,0:T(8,128)(2,1)}), bf16[16,64,384]{2,1,0:T(8,128)(2,1)S(1)}, u32[]{:S(2)}, u32[]{:S(2)}) %all-to-all-start.1) | async-done | bytes 786464 | tf_op jit(solution)/shard_map/all_to_all | solution.py:130
  271.1 1.0 convolution_convert_fusion.5
  272.2 1.0 convolution_convert_fusion.4
  (78 shorter events, 18.9 us)
Async XLA Ops:
  7.2 123.5 %copy-start = (bf16[1,6144,128]{2,1,0:T(8,128)(2,1)S(1)}, bf16[1,6144,128]{2,1,0:T(8,128)(2,1)}, u32[]{:S(2)}) copy-start(bf16[1,6144,128]{2,1,0:T(8,128)(2,1)} %param.11) | copy-start | bytes 4718596
  10.7 117.3 %copy-start.4 = (bf16[1,128,6144]{2,1,0:T(8,128)(2,1)S(1)}, bf16[1,128,6144]{2,1,0:T(8,128)(2,1)}, u32[]{:S(2)}) copy-start(bf16[1,128,6144]{2,1,0:T(8,128)(2,1)} %param.12) | copy-start | bytes 4718596
  13.1 21.4 %all-to-all-start = ((bf16[16,64,384]{2,1,0:T(8,128)(2,1)}), bf16[16,64,384]{2,1,0:T(8,128)(2,1)}, u32[]{:S(2)}, u32[]{:S(2)}) async-start(bf16[16,64,384]{2,1,0:T(8,128)(2,1)} %pad_maximum_fusion.1), calls=%async_computation | async-start | bytes 1572864 | tf_op jit(solution)/shard_map/all_to_all | solution.py:55
  19.3 98.4 %all-gather.2.cloned.1.call-start = ((), (), s32[]{:S(2)}) async-start(), calls=%async_computation.3 | async-start | bytes 6684672 | tf_op jit(solution)/shard_map/all_gather | solution.py:59
  36.4 210.1 %reduce-scatter.4.cloned.1.call-start = ((), (), s32[]{:S(2)}) async-start(), calls=%async_computation.4 | async-start | bytes 6684672
  117.6 11.4 %copy-start.5 = (bf16[1,6144,128]{2,1,0:T(8,128)(2,1)S(1)}, bf16[1,6144,128]{2,1,0:T(8,128)(2,1)}, u32[]{:S(2)}) copy-start(bf16[1,6144,128]{2,1,0:T(8,128)(2,1)} %param.10) | copy-start | bytes 4718596
  117.6 10.4 %collective-permute-start = (bf16[2,256,6144]{2,1,0:T(8,128)(2,1)}, bf16[2,256,6144]{2,1,0:T(8,128)(2,1)S(1)}, u32[]{:S(2)}, u32[]{:S(2)}) collective-permute-start(bf16[2,256,6144]{2,1,0:T(8,128)(2,1)} %all-gather.2.cloned.1.call-done), channel_id=1, source_target_pairs={{0,16},{16,0},{32,48},{48,32},{64,80},{80,64},{96,112},{112,96},{1... | collective-permute-start | bytes 18874376 | tf_op jit(solution)/shard_map/ppermute | solution.py:60
  128.0 2.6 copy-start.3
  131.7 2.0 copy-start.6
  133.7 4.3 %slice-start.2 = ((s8[6291456]{0:T(1024)(128)(4,1)}), s8[4194304]{0:T(1024)(128)(4,1)S(1)}, s32[]{:S(2)}) async-start(s8[6291456]{0:T(1024)(128)(4,1)} %bitcast.127), calls=%async_computation.7 | async-start | bytes 8388608
  134.7 3.3 %slice-start.3 = ((s8[6291456]{0:T(1024)(128)(4,1)}), s8[2097152]{0:T(1024)(128)(4,1)S(1)}, s32[]{:S(2)}) async-start(s8[6291456]{0:T(1024)(128)(4,1)} %bitcast.127), calls=%async_computation.8 | async-start | bytes 4194304
  137.9 10.4 %collective-permute-start.1 = (bf16[2,6144,256]{1,2,0:T(8,128)(2,1)}, bf16[2,6144,256]{1,2,0:T(8,128)(2,1)S(1)}, u32[]{:S(2)}, u32[]{:S(2)}) collective-permute-start(bf16[2,6144,256]{1,2,0:T(8,128)(2,1)} %pad_maximum_fusion), channel_id=1, source_target_pairs={{0,16},{16,0},{32,48},{48,32},{64,80},{80,64},{96,112},{112,96},{1... | collective-permute-start | bytes 18874376 | tf_op jit(solution)/shard_map/ppermute | solution.py:98
  141.0 2.0 copy-start.12
  141.0 2.0 copy-start.14
  141.0 2.0 copy-start.10
  162.1 4.3 %copy-start.13 = (bf16[256,128]{1,0:T(8,128)(2,1)S(1)}, bf16[256,128]{1,0:T(8,128)(2,1)}, u32[]{:S(2)}) copy-start(bf16[256,128]{1,0:T(8,128)(2,1)} %copy-done.12) | copy-start | bytes 196612
  166.4 4.8 %copy-start.11 = (bf16[256,128]{1,0:T(8,128)(2,1)S(1)}, bf16[256,128]{1,0:T(8,128)(2,1)}, u32[]{:S(2)}) copy-start(bf16[256,128]{1,0:T(8,128)(2,1)} %copy-done.10) | copy-start | bytes 196612
  166.4 7.9 %slice-start = ((s8[6291456]{0:T(1024)(128)(4,1)}), s8[4194304]{0:T(1024)(128)(4,1)S(1)}, s32[]{:S(2)}) async-start(s8[6291456]{0:T(1024)(128)(4,1)} %bitcast.125), calls=%async_computation.5 | async-start | bytes 8388608
  171.2 3.1 %slice-start.1 = ((s8[6291456]{0:T(1024)(128)(4,1)}), s8[2097152]{0:T(1024)(128)(4,1)S(1)}, s32[]{:S(2)}) async-start(s8[6291456]{0:T(1024)(128)(4,1)} %bitcast.125), calls=%async_computation.6 | async-start | bytes 4194304
  171.2 3.1 %copy-start.9 = (bf16[256,128]{1,0:T(8,128)(2,1)S(1)}, bf16[256,128]{1,0:T(8,128)(2,1)}, u32[]{:S(2)}) copy-start(bf16[256,128]{1,0:T(8,128)(2,1)} %copy-done.8) | copy-start | bytes 196612
  176.5 79.3 %copy-start.7 = (bf16[256,128]{1,0:T(8,128)(2,1)S(1)}, bf16[256,128]{1,0:T(8,128)(2,1)}, u32[]{:S(2)}) copy-start(bf16[256,128]{1,0:T(8,128)(2,1)} %copy-done.6) | copy-start | bytes 196612
  249.5 21.5 %all-to-all-start.1 = ((bf16[16,64,384]{2,1,0:T(8,128)(2,1)}), bf16[16,64,384]{2,1,0:T(8,128)(2,1)S(1)}, u32[]{:S(2)}, u32[]{:S(2)}) async-start(bf16[16,64,384]{2,1,0:T(8,128)(2,1)} %maximum_dynamic-update-slice_fusion), calls=%async_computation.1 | async-start | bytes 1572864 | tf_op jit(solution)/shard_map/all_to_all | solution.py:130
  255.9 4.8 %copy-start.2 = (f32[6144,128]{1,0:T(8,128)S(1)}, f32[6144,128]{1,0:T(8,128)}, u32[]{:S(2)}) copy-start(f32[6144,128]{1,0:T(8,128)} %fusion.17) | copy-start | bytes 9437188
  260.6 12.6 %copy-start.1 = (bf16[1,6144,128]{2,1,0:T(8,128)(2,1)S(1)}, bf16[1,6144,128]{2,1,0:T(8,128)(2,1)}, u32[]{:S(2)}) copy-start(bf16[1,6144,128]{2,1,0:T(8,128)(2,1)} %param.11) | copy-start | bytes 4718596
  (2 other events, 2.8 us)
Sparse Core Ops, SparseCore 0:
  36.5 81.1 all-gather.1
  161.4 85.0 reduce-scatter.3

commit v3 on v2

--- a/solution.py
+++ b/solution.py
@@ -1,10 +1,13 @@
 import jax
 import jax.numpy as jnp
 from jax import lax
-from jax.sharding import PartitionSpec as P
+from jax.sharding import Mesh, NamedSharding, PartitionSpec as P
 
 EXPERTS = 4
 CAP = 32
+DP = ("y", "xhi", "core")
+TN = ("xlo", "z")
+SRC = ("y", "xhi")
 
 
 precise = lax.Precision.HIGHEST
@@ -25,11 +28,8 @@
 
 def per_device(tokens, routes, gate_weights, gate_matrix, up_matrix, down_matrix, cotangent):
     feature_cols = tokens.shape[1]
-    n_dp = lax.axis_size("dp")
-    expert_span = n_dp // EXPERTS
-    half = n_dp // 2
-    core = lax.axis_index("dp") % 2
-    pair = [(d, d ^ 1) for d in range(n_dp)]
+    n_src = lax.axis_size(SRC)
+    expert_span = n_src // EXPERTS
     onehot, weights = slot_tables(routes, gate_weights, CAP)
     member = onehot.astype(jnp.float32)
     scaled = member * weights[:, :, None]
@@ -49,15 +49,15 @@
         "tr,tc->rc", scaled_wide, cotangent.astype(jnp.float32), precision=precise
     ).astype(jnp.bfloat16)
     send = jnp.concatenate(
-        [token_send.reshape(n_dp, CAP, feature_cols), grad_send.reshape(n_dp, CAP, feature_cols)],
+        [token_send.reshape(n_src, CAP, feature_cols), grad_send.reshape(n_src, CAP, feature_cols)],
         axis=1,
     )
-    recv = lax.all_to_all(send, "dp", split_axis=0, concat_axis=0, tiled=True)
-    mine = lax.dynamic_slice_in_dim(recv, core * half, half, axis=0)
-    mine = mine.reshape(half, 2, CAP, feature_cols).transpose(1, 0, 2, 3)
-    mine = mine.reshape(2, half * CAP, feature_cols)
-    mine_full = lax.all_gather(mine, "tensor", axis=2, tiled=True)
-    other_full = lax.ppermute(mine_full, "dp", pair)
+    recv = lax.all_to_all(send, SRC, split_axis=0, concat_axis=0, tiled=True)
+    mine = recv.reshape(n_src, 2, CAP, feature_cols).transpose(1, 0, 2, 3)
+    mine = mine.reshape(2, n_src * CAP, feature_cols)
+    mine_full = lax.all_gather(mine, TN, axis=2, tiled=True)
+    pair = [(0, 1), (1, 0)]
+    other_full = lax.ppermute(mine_full, "core", pair)
 
     gate_local = gate_matrix[0]
     up_local = up_matrix[0]
@@ -95,14 +95,13 @@
 
     ga, ua, back_a = backward(rows_a, grads_a, *fa[:4])
     gb, ub, back_b = backward(rows_b, grads_b, *fb[:4])
-    partner = lax.ppermute(jnp.stack([fb[5], back_b]), "dp", pair)
-    own = jnp.stack([fa[5], back_a], axis=1)
-    summed = own.astype(jnp.float32) + partner.transpose(1, 0, 2).astype(jnp.float32)
-    summed = summed.astype(jnp.bfloat16).reshape(own.shape[0], -1)
-    scattered = lax.psum_scatter(summed, "tensor", scatter_dimension=0, tiled=True)
-    scattered = scattered.reshape(scattered.shape[0], 2, -1)
-    out_rows = scattered[:, 0].T
-    back_rows = scattered[:, 1].T
+    partner = lax.ppermute(jnp.concatenate([fb[5], back_b], axis=1), "core", pair)
+    own = jnp.concatenate([fa[5], back_a], axis=1)
+    summed = (own.astype(jnp.float32) + partner.astype(jnp.float32)).astype(jnp.bfloat16)
+    scattered = lax.psum_scatter(summed, TN, scatter_dimension=0, tiled=True)
+    n_rows = fa[5].shape[1]
+    out_rows = scattered[:, :n_rows].T
+    back_rows = scattered[:, n_rows:].T
 
     gate_gradient = (
         jnp.einsum("rd,rh->dh", rows_a, ga, preferred_element_type=jnp.float32)
@@ -119,15 +118,12 @@
 
     done = jnp.concatenate(
         [
-            out_rows.reshape(half, CAP, feature_cols),
-            back_rows.reshape(half, CAP, feature_cols),
+            out_rows.reshape(n_src, CAP, feature_cols),
+            back_rows.reshape(n_src, CAP, feature_cols),
         ],
         axis=1,
     )
-    ret_send = lax.dynamic_update_slice_in_dim(
-        jnp.zeros((n_dp, 2 * CAP, feature_cols), jnp.bfloat16), done, core * half, axis=0
-    )
-    returned = lax.all_to_all(ret_send, "dp", split_axis=0, concat_axis=0, tiled=True).astype(
+    returned = lax.all_to_all(done, SRC, split_axis=0, concat_axis=0, tiled=True).astype(
         jnp.float32
     )
     returned_out = returned[:, :CAP].reshape(-1, feature_cols)
@@ -142,22 +138,44 @@
 
 
 def solution(mesh):
+    sizes = dict(mesh.shape)
+    sub = Mesh(
+        mesh.devices.reshape(
+            sizes["dp"] // 4, 2, 2, 2, sizes["tensor"] // 2
+        ),
+        DP + TN,
+    )
     in_specs = (
-        P("dp", "tensor"),
-        P("dp", None),
-        P("dp", None),
-        P("dp", None, "tensor"),
-        P("dp", None, "tensor"),
-        P("dp", "tensor", None),
-        P("dp", "tensor"),
+        P(DP, TN),
+        P(DP, None),
+        P(DP, None),
+        P(DP, None, TN),
+        P(DP, None, TN),
+        P(DP, TN, None),
+        P(DP, TN),
     )
     out_specs = (
+        P(DP, TN),
+        P(DP, TN),
+        P(DP, None, TN),
+        P(DP, None, TN),
+        P(DP, TN, None),
+    )
+    placed = (
         P("dp", "tensor"),
         P("dp", "tensor"),
         P("dp", None, "tensor"),
         P("dp", None, "tensor"),
         P("dp", "tensor", None),
     )
-    return jax.shard_map(
-        per_device, mesh=mesh, in_specs=in_specs, out_specs=out_specs, check_vma=False
+    inner = jax.shard_map(
+        per_device, mesh=sub, in_specs=in_specs, out_specs=out_specs, check_vma=False
     )
+
+    def run(*args):
+        outs = inner(*args)
+        return tuple(
+            lax.with_sharding_constraint(o, NamedSharding(mesh, p)) for o, p in zip(outs, placed)
+        )
+
+    return run

time: 282 us -> 271 us (0.961)
  waiting for transfers between devices: 187 us -> 170 us
  blocking collectives: 0 us -> 16.1 us
  starting transfers between devices: 12.7 us -> 6.26 us
    all_to_all x2 -> x1, waiting for transfers between devices: 21.3 us -> 4.77 us  [per_device(): lax.all_to_all(done, SRC, split_axis=0, concat_axis=0, tiled=True)]
    all_to_all x0 -> x1, blocking collectives: none -> 16.1 us  [per_device(): recv = lax.all_to_all(send, SRC, split_axis=0, concat_axis=0, tiled=True)]
    all_to_all x2 -> x1, starting transfers between devices: 12.5 us -> 6.05 us  [per_device(): lax.all_to_all(done, SRC, split_axis=0, concat_axis=0, tiled=True)]
    concatenate x1 -> x3, other arithmetic: 1.01 us -> 6.21 us  [the longest x1 5.38 us: per_device(): jnp.concatenate([fb[5], back_b], axis=1)]
    another operation x1 -> x0, other arithmetic: 3.13 us -> none  [per_device(): partner = lax.ppermute(jnp.stack([fb[5], back_b]), 'dp', pair)]
    unnamed x42 -> x35, local copies, waits for them, and re-layouts: 11.3 us -> 10.7 us
  transfers between devices with their start and end apart: 6 -> 5, of which waited for: 6 -> 5; matrix products, arithmetic and copies ran while one was open for 10% -> 10% of each run, Pallas kernels for 0% -> 0%
where the time goes in v3:
time: 271 us; the launch traced here: 270 us
  waiting for transfers between devices  170 us (63%)
  matrix products  37.2 us (14%)
  blocking collectives  16.1 us (6%)
  between operations  14.3 us (5%)
  other arithmetic  13.1 us (5%)
  local copies, waits for them, and re-layouts  12.8 us (5%)
  starting transfers between devices  6.26 us (2%)
    all_gather x1, waiting for transfers between devices, per_device(): mine_full = lax.all_gather(mine, TN, axis=2, tiled=True)  81.7 us
    unnamed x3, waiting for transfers between devices  69.4 us
    all_to_all x1, blocking collectives, per_device(): recv = lax.all_to_all(send, SRC, split_axis=0, concat_axis=0, tiled=True)  16.1 us
    unnamed x35, local copies, waits for them, and re-layouts  10.7 us
    ppermute x1, waiting for transfers between devices, per_device(): other_full = lax.ppermute(mine_full, 'core', pair)  10.4 us
    all_to_all x1, starting transfers between devices, per_device(): lax.all_to_all(done, SRC, split_axis=0, concat_axis=0, tiled=True)  6.05 us
  transfers between devices with their start and end apart: 5, of which 5 were waited for; matrix products, arithmetic and copies ran while one was open for 10% of the time, Pallas kernels for 0%

profile of v3, /device:TPU:2, one launch (start us, length us, event | category | flops | bytes accessed | tf_op | source)
XLA Modules:
  0.0 269.9 jit_solution(16011174447645806509)
XLA Ops:
  10.8 1.1 convolution_convert_fusion.3
  11.9 16.1 %all_to_all.10 = bf16[8,64,384]{2,1,0:T(8,128)(2,1)S(1)} all-to-all(bf16[8,64,384]{2,1,0:T(8,128)(2,1)S(1)} %pad_maximum_fusion.1), channel_id=1, replica_groups=mesh['y'=4,'xhi'=2,'core'=2,'xlo'=2,'z'=8] {'y','xhi'}, dimensions={0} | all-to-all | bytes 786432 | tf_op jit(solution)/shard_map/all_to_all | solution.py:55
  28.9 81.7 %all-gather.2.cloned.1.call-done = bf16[2,256,6144]{2,1,0:T(8,128)(2,1)} async-done(((bf16[2,256,384]{2,1,0:T(8,128)(2,1)}), bf16[2,256,6144]{2,1,0:T(8,128)(2,1)}) %all-gather.2.cloned.1.call-update) | async-done | bytes 6291472 | tf_op jit(solution)/shard_map/all_gather | solution.py:58
  110.5 10.4 %collective-permute-done = bf16[2,256,6144]{2,1,0:T(8,128)(2,1)S(1)} collective-permute-done((bf16[2,256,6144]{2,1,0:T(8,128)(2,1)}, bf16[2,256,6144]{2,1,0:T(8,128)(2,1)S(1)}, u32[]{:S(2)}, u32[]{:S(2)}) %collective-permute-start) | collective-permute-done | bytes 6291488 | tf_op jit(solution)/shard_map/ppermute | solution.py:60
  120.9 1.0 fusion.14
  121.9 1.0 fusion.20
  123.6 1.0 multiply_convert_fusion.2
  126.6 2.7 %fusion.4 = bf16[6144,256]{0,1:T(8,128)(2,1)} fusion(f32[256,6144]{1,0:T(8,128)S(1)} %fusion.29, bf16[256,128]{1,0:T(8,128)(2,1)S(1)} %get-tuple-element.14, bf16[1,6144,128]{2,1,0:T(8,128)(2,1)S(1)} %copy-done), kind=kOutput, calls=%fused_computation.12 | convolution fusion | flops 405798912 | bytes 11075584 | tf_op jit(solution)/shard_map/dh,rh->dr/dot_general | solution.py:87
  129.3 5.4 %pad_maximum_fusion = bf16[6144,512]{0,1:T(8,128)(2,1)} fusion(bf16[6144,256]{0,1:T(8,128)(2,1)} %fusion.4, bf16[6144,256]{0,1:T(8,128)(2,1)S(1)} %fusion.3), kind=kLoop, calls=%fused_computation.20 | loop fusion | flops 12582912 | bytes 12582912 | tf_op jit(solution)/shard_map/concatenate | solution.py:98
  136.1 1.0 fusion.18
  140.2 1.0 fusion.5
  141.2 3.9 %collective-permute-done.1 = bf16[6144,512]{0,1:T(8,128)(2,1)S(1)} collective-permute-done((bf16[6144,512]{0,1:T(8,128)(2,1)}, bf16[6144,512]{0,1:T(8,128)(2,1)S(1)}, u32[]{:S(2)}, u32[]{:S(2)}) %collective-permute-start.1) | collective-permute-done | bytes 6291488 | tf_op jit(solution)/shard_map/ppermute | solution.py:98
  145.1 4.6 %add_convert_fusion = bf16[6144,512]{0,1:T(8,128)(2,1)} fusion(bf16[6144,512]{0,1:T(8,128)(2,1)S(1)} %collective-permute-done.1, bf16[6144,256]{0,1:T(8,128)(2,1)S(1)} %fusion.5, bf16[6144,256]{0,1:T(8,128)(2,1)S(1)} %fusion.2), kind=kLoop, calls=%fused_computation | loop fusion | flops 22020096 | bytes 18874368 | tf_op jit(solution)/shard_map/convert_element_type | solution.py:100
  149.6 8.6 %copy.31 = bf16[6144,512]{1,0:T(8,128)(2,1)} copy(bf16[6144,512]{0,1:T(8,128)(2,1)} %add_convert_fusion) | data formatting | bytes 12582912
  159.0 4.2 %fusion.12 = f32[128,6144]{1,0:T(8,128)} fusion(bf16[256,128]{1,0:T(8,128)(2,1)S(1)} %copy-done.11, bf16[2,256,6144]{2,1,0:T(8,128)(2,1)} %all-gather.2.cloned.1.call-done), kind=kOutput, calls=%fused_computation.25 | convolution fusion | flops 402653184 | bytes 6356992 | tf_op jit(solution)/shard_map/rh,rd->hd/dot_general | solution.py:115
  163.3 3.1 %fusion.16 = f32[6144,128]{1,0:T(8,128)S(1)} fusion(bf16[256,128]{1,0:T(8,128)(2,1)S(1)} %copy-done.9, bf16[2,256,6144]{2,1,0:T(8,128)(2,1)} %all-gather.2.cloned.1.call-done), kind=kOutput, calls=%fused_computation.29 | convolution fusion | flops 402653184 | bytes 6356992 | tf_op jit(solution)/shard_map/rd,rh->dh/dot_general | solution.py:107
  166.4 3.3 %fusion.15 = f32[6144,128]{1,0:T(8,128)S(1)} fusion(bf16[256,128]{1,0:T(8,128)(2,1)S(1)} %copy-done.7, bf16[2,256,6144]{2,1,0:T(8,128)(2,1)} %all-gather.2.cloned.1.call-done), kind=kOutput, calls=%fused_computation.28 | convolution fusion | flops 402653184 | bytes 6356992 | tf_op jit(solution)/shard_map/rd,rh->dh/dot_general | solution.py:111
  169.7 2.2 fusion.10
  171.9 2.2 fusion.11
  174.1 69.4 %reduce-scatter.4.cloned.1.call-done = bf16[384,512]{1,0:T(8,128)(2,1)} async-done(((bf16[6144,512]{1,0:T(8,128)(2,1)}), bf16[384,512]{1,0:T(8,128)(2,1)}) %reduce-scatter.4.cloned.1.call-update) | async-done | bytes 393232
  243.5 1.0 fusion.42
  245.6 6.0 %all-to-all-start.1 = ((bf16[8,64,384]{2,1,0:T(8,128)(2,1)}), bf16[8,64,384]{2,1,0:T(8,128)(2,1)S(1)}, u32[]{:S(2)}, u32[]{:S(2)}) async-start(bf16[8,64,384]{2,1,0:T(8,128)(2,1)} %pad_maximum_fusion.2), calls=%async_computation.1 | async-start | bytes 786432 | tf_op jit(solution)/shard_map/all_to_all | solution.py:126
  251.7 4.7 %fusion.9 = bf16[1,128,6144]{2,1,0:T(8,128)(2,1)} fusion(f32[128,6144]{1,0:T(8,128)} %fusion.12, bf16[256,128]{1,0:T(8,128)(2,1)S(1)} %get-tuple-element.12, bf16[2,256,6144]{2,1,0:T(8,128)(2,1)} %copy-done.2), kind=kOutput, calls=%fused_computation.17 | convolution fusion | flops 404226048 | bytes 7929856 | tf_op jit(solution)/shard_map/rh,rd->hd/dot_general | solution.py:116
  256.4 4.8 %all-to-all-done.1 = bf16[8,64,384]{2,1,0:T(8,128)(2,1)S(1)} async-done(((bf16[8,64,384]{2,1,0:T(8,128)(2,1)}), bf16[8,64,384]{2,1,0:T(8,128)(2,1)S(1)}, u32[]{:S(2)}, u32[]{:S(2)}) %all-to-all-start.1) | async-done | bytes 393248 | tf_op jit(solution)/shard_map/all_to_all | solution.py:126
  (68 shorter events, 15.2 us)
Async XLA Ops:
  7.2 116.4 %copy-start = (bf16[1,6144,128]{2,1,0:T(8,128)(2,1)S(1)}, bf16[1,6144,128]{2,1,0:T(8,128)(2,1)}, u32[]{:S(2)}) copy-start(bf16[1,6144,128]{2,1,0:T(8,128)(2,1)} %param.11) | copy-start | bytes 4718596
  7.2 113.7 %copy-start.3 = (bf16[1,128,6144]{2,1,0:T(8,128)(2,1)S(1)}, bf16[1,128,6144]{2,1,0:T(8,128)(2,1)}, u32[]{:S(2)}) copy-start(bf16[1,128,6144]{2,1,0:T(8,128)(2,1)} %param.12) | copy-start | bytes 4718596
  7.2 103.3 %all-gather.2.cloned.1.call-start = ((), (), s32[]{:S(2)}) async-start(), calls=%async_computation.3 | async-start | bytes 6684672 | tf_op jit(solution)/shard_map/all_gather | solution.py:58
  28.8 214.6 %reduce-scatter.4.cloned.1.call-start = ((), (), s32[]{:S(2)}) async-start(), calls=%async_computation.4 | async-start | bytes 6684672
  110.5 11.4 %copy-start.4 = (bf16[1,6144,128]{2,1,0:T(8,128)(2,1)S(1)}, bf16[1,6144,128]{2,1,0:T(8,128)(2,1)}, u32[]{:S(2)}) copy-start(bf16[1,6144,128]{2,1,0:T(8,128)(2,1)} %param.10) | copy-start | bytes 4718596
  110.5 10.4 %collective-permute-start = (bf16[2,256,6144]{2,1,0:T(8,128)(2,1)}, bf16[2,256,6144]{2,1,0:T(8,128)(2,1)S(1)}, u32[]{:S(2)}, u32[]{:S(2)}) collective-permute-start(bf16[2,256,6144]{2,1,0:T(8,128)(2,1)} %all-gather.2.cloned.1.call-done), channel_id=1, source_target_pairs={{0,16},{16,0},{1,17},{17,1},{2,18},{18,2},{3,19},{19,3},{4,20},{20... | collective-permute-start | bytes 18874376 | tf_op jit(solution)/shard_map/ppermute | solution.py:60
  120.9 2.7 copy-start.2
  126.6 8.3 %slice-start.2 = ((s8[6291456]{0:T(1024)(128)(4,1)}), s8[4194304]{0:T(1024)(128)(4,1)S(1)}, s32[]{:S(2)}) async-start(s8[6291456]{0:T(1024)(128)(4,1)} %bitcast.109), calls=%async_computation.7 | async-start | bytes 8388608
  129.3 5.5 %slice-start.3 = ((s8[6291456]{0:T(1024)(128)(4,1)}), s8[2097152]{0:T(1024)(128)(4,1)S(1)}, s32[]{:S(2)}) async-start(s8[6291456]{0:T(1024)(128)(4,1)} %bitcast.109), calls=%async_computation.8 | async-start | bytes 4194304
  134.7 1.4 copy-start.5
  134.7 10.4 %collective-permute-start.1 = (bf16[6144,512]{0,1:T(8,128)(2,1)}, bf16[6144,512]{0,1:T(8,128)(2,1)S(1)}, u32[]{:S(2)}, u32[]{:S(2)}) collective-permute-start(bf16[6144,512]{0,1:T(8,128)(2,1)} %pad_maximum_fusion), channel_id=1, source_target_pairs={{0,16},{16,0},{1,17},{17,1},{2,18},{18,2},{3,19},{19,3},{4,20},{20... | collective-permute-start | bytes 18874376 | tf_op jit(solution)/shard_map/ppermute | solution.py:98
  138.1 2.0 copy-start.8
  138.1 2.0 copy-start.10
  138.1 2.0 copy-start.6
  158.2 0.8 copy-start.11
  159.0 4.2 %copy-start.9 = (bf16[256,128]{1,0:T(8,128)(2,1)S(1)}, bf16[256,128]{1,0:T(8,128)(2,1)}, u32[]{:S(2)}) copy-start(bf16[256,128]{1,0:T(8,128)(2,1)} %copy-done.8) | copy-start | bytes 196612
  163.3 3.1 %copy-start.7 = (bf16[256,128]{1,0:T(8,128)(2,1)S(1)}, bf16[256,128]{1,0:T(8,128)(2,1)}, u32[]{:S(2)}) copy-start(bf16[256,128]{1,0:T(8,128)(2,1)} %copy-done.6) | copy-start | bytes 196612
  163.3 6.4 %slice-start = ((s8[6291456]{0:T(1024)(128)(4,1)}), s8[4194304]{0:T(1024)(128)(4,1)S(1)}, s32[]{:S(2)}) async-start(s8[6291456]{0:T(1024)(128)(4,1)} %bitcast.107), calls=%async_computation.5 | async-start | bytes 8388608
  166.4 3.3 %slice-start.1 = ((s8[6291456]{0:T(1024)(128)(4,1)}), s8[2097152]{0:T(1024)(128)(4,1)S(1)}, s32[]{:S(2)}) async-start(s8[6291456]{0:T(1024)(128)(4,1)} %bitcast.107), calls=%async_computation.6 | async-start | bytes 4194304
  245.6 15.5 %all-to-all-start.1 = ((bf16[8,64,384]{2,1,0:T(8,128)(2,1)}), bf16[8,64,384]{2,1,0:T(8,128)(2,1)S(1)}, u32[]{:S(2)}, u32[]{:S(2)}) async-start(bf16[8,64,384]{2,1,0:T(8,128)(2,1)} %pad_maximum_fusion.2), calls=%async_computation.1 | async-start | bytes 786432 | tf_op jit(solution)/shard_map/all_to_all | solution.py:126
  251.7 11.4 %copy-start.1 = (bf16[1,6144,128]{2,1,0:T(8,128)(2,1)S(1)}, bf16[1,6144,128]{2,1,0:T(8,128)(2,1)}, u32[]{:S(2)}) copy-start(bf16[1,6144,128]{2,1,0:T(8,128)(2,1)} %param.11) | copy-start | bytes 4718596
Sparse Core Ops, SparseCore 0:
  28.9 81.5 all-gather.1
  158.3 85.0 reduce-scatter.3

commit v4 on v3

--- a/solution.py
+++ b/solution.py
@@ -1,6 +1,7 @@
 import jax
 import jax.numpy as jnp
 from jax import lax
+from jax.experimental.layout import Layout, with_layout_constraint
 from jax.sharding import Mesh, NamedSharding, PartitionSpec as P
 
 EXPERTS = 4
@@ -72,6 +73,7 @@
         out_t = jnp.einsum(
             "hd,rh->dr", down_local, hidden, preferred_element_type=jnp.float32
         ).astype(jnp.bfloat16)
+        out_t = with_layout_constraint(out_t, Layout(major_to_minor=(0, 1)))
         return gate_pre, up_pre, sigmoid_gate, activated, hidden, out_t
 
     def backward(rows, grads, gate_pre, up_pre, sigmoid_gate, activated):
@@ -86,6 +88,7 @@
             jnp.einsum("dh,rh->dr", gate_local, gate_grad, preferred_element_type=jnp.float32)
             + jnp.einsum("dh,rh->dr", up_local, up_grad, preferred_element_type=jnp.float32)
         ).astype(jnp.bfloat16)
+        back_t = with_layout_constraint(back_t, Layout(major_to_minor=(0, 1)))
         return gate_grad, up_grad, back_t
 
     rows_a, grads_a = mine_full[0], mine_full[1]

time: 271 us -> 261 us (0.963)
  local copies, waits for them, and re-layouts: 12.8 us -> 4.14 us
    reduce_scatter x0 -> x1, waiting for transfers between devices: none -> 69.6 us  [per_device(): scattered = lax.psum_scatter(summed, TN, scatter_dimension=0, tiled=True)]
    unnamed x3 -> x2, waiting for transfers between devices: 69.4 us -> 0.03 us
    unnamed x35 -> x32, local copies, waits for them, and re-layouts: 10.7 us -> 1.74 us
where the time goes in v4:
time: 261 us; the launch traced here: 260 us
  waiting for transfers between devices  170 us (65%)
  matrix products  37.1 us (14%)
  blocking collectives  16.1 us (6%)
  between operations  14.3 us (5%)
  other arithmetic  12 us (5%)
  starting transfers between devices  5.97 us (2%)
  local copies, waits for them, and re-layouts  4.14 us (2%)
    all_gather x1, waiting for transfers between devices, per_device(): mine_full = lax.all_gather(mine, TN, axis=2, tiled=True)  81.7 us
    reduce_scatter x1, waiting for transfers between devices, per_device(): scattered = lax.psum_scatter(summed, TN, scatter_dimension=0, tiled=True)  69.6 us
    all_to_all x1, blocking collectives, per_device(): recv = lax.all_to_all(send, SRC, split_axis=0, concat_axis=0, tiled=True)  16.1 us
    ppermute x1, waiting for transfers between devices, per_device(): other_full = lax.ppermute(mine_full, 'core', pair)  10.4 us
    all_to_all x1, starting transfers between devices, per_device(): lax.all_to_all(done, SRC, split_axis=0, concat_axis=0, tiled=True)  5.75 us
  transfers between devices with their start and end apart: 5, of which 5 were waited for; matrix products, arithmetic and copies ran while one was open for 10% of the time, Pallas kernels for 0%

profile of v4, /device:TPU:2, one launch (start us, length us, event | category | flops | bytes accessed | tf_op | source)
XLA Modules:
  0.0 260.2 jit_solution(12670048209112556618)
XLA Ops:
  10.8 1.1 convolution_convert_fusion.3
  11.9 16.1 %all_to_all.10 = bf16[8,64,384]{2,1,0:T(8,128)(2,1)S(1)} all-to-all(bf16[8,64,384]{2,1,0:T(8,128)(2,1)S(1)} %pad_maximum_fusion.1), channel_id=1, replica_groups=mesh['y'=4,'xhi'=2,'core'=2,'xlo'=2,'z'=8] {'y','xhi'}, dimensions={0} | all-to-all | bytes 786432 | tf_op jit(solution)/shard_map/all_to_all | solution.py:56
  28.9 81.7 %all-gather.2.cloned.1.call-done = bf16[2,256,6144]{2,1,0:T(8,128)(2,1)} async-done(((bf16[2,256,384]{2,1,0:T(8,128)(2,1)}), bf16[2,256,6144]{2,1,0:T(8,128)(2,1)}) %all-gather.2.cloned.1.call-update) | async-done | bytes 6291472 | tf_op jit(solution)/shard_map/all_gather | solution.py:59
  110.5 10.4 %collective-permute-done = bf16[2,256,6144]{2,1,0:T(8,128)(2,1)S(1)} collective-permute-done((bf16[2,256,6144]{2,1,0:T(8,128)(2,1)}, bf16[2,256,6144]{2,1,0:T(8,128)(2,1)S(1)}, u32[]{:S(2)}, u32[]{:S(2)}) %collective-permute-start) | collective-permute-done | bytes 6291488 | tf_op jit(solution)/shard_map/ppermute | solution.py:61
  120.9 1.0 fusion.14
  121.9 1.1 fusion.20
  123.6 1.0 multiply_convert_fusion.2
  124.6 1.0 fusion.3
  126.6 2.7 %fusion.4 = bf16[6144,256]{1,0:T(8,128)(2,1)} fusion(f32[256,6144]{0,1:T(8,128)S(1)} %fusion.29, bf16[256,128]{1,0:T(8,128)(2,1)S(1)} %get-tuple-element.14, bf16[1,6144,128]{2,1,0:T(8,128)(2,1)S(1)} %copy-done), kind=kOutput, calls=%fused_computation.12 | convolution fusion | flops 405798912 | bytes 11075584 | tf_op jit(solution)/shard_map/dh,rh->dr/dot_general | solution.py:89
  129.3 5.1 %pad_maximum_fusion = bf16[6144,512]{1,0:T(8,128)(2,1)} fusion(bf16[6144,256]{1,0:T(8,128)(2,1)} %fusion.4, bf16[6144,256]{1,0:T(8,128)(2,1)S(1)} %fusion.3), kind=kLoop, calls=%fused_computation.20 | loop fusion | flops 12582912 | bytes 12582912 | tf_op jit(solution)/shard_map/concatenate | solution.py:101
  137.8 1.0 fusion.2
  139.8 1.0 fusion.5
  140.8 4.0 %collective-permute-done.1 = bf16[6144,512]{1,0:T(8,128)(2,1)S(1)} collective-permute-done((bf16[6144,512]{1,0:T(8,128)(2,1)}, bf16[6144,512]{1,0:T(8,128)(2,1)S(1)}, u32[]{:S(2)}, u32[]{:S(2)}) %collective-permute-start.1) | collective-permute-done | bytes 6291488 | tf_op jit(solution)/shard_map/ppermute | solution.py:101
  144.7 3.8 %add_convert_fusion = bf16[6144,512]{1,0:T(8,128)(2,1)} fusion(bf16[6144,512]{1,0:T(8,128)(2,1)S(1)} %collective-permute-done.1, bf16[6144,256]{1,0:T(8,128)(2,1)S(1)} %fusion.5, bf16[6144,256]{1,0:T(8,128)(2,1)S(1)} %fusion.2), kind=kLoop, calls=%fused_computation | loop fusion | flops 22020096 | bytes 18874368 | tf_op jit(solution)/shard_map/convert_element_type | solution.py:103
  149.3 4.2 %fusion.12 = f32[128,6144]{1,0:T(8,128)} fusion(bf16[256,128]{1,0:T(8,128)(2,1)S(1)} %copy-done.11, bf16[2,256,6144]{2,1,0:T(8,128)(2,1)} %all-gather.2.cloned.1.call-done), kind=kOutput, calls=%fused_computation.25 | convolution fusion | flops 402653184 | bytes 6356992 | tf_op jit(solution)/shard_map/rh,rd->hd/dot_general | solution.py:118
  153.6 3.1 %fusion.16 = f32[6144,128]{1,0:T(8,128)S(1)} fusion(bf16[256,128]{1,0:T(8,128)(2,1)S(1)} %copy-done.9, bf16[2,256,6144]{2,1,0:T(8,128)(2,1)} %all-gather.2.cloned.1.call-done), kind=kOutput, calls=%fused_computation.29 | convolution fusion | flops 402653184 | bytes 6356992 | tf_op jit(solution)/shard_map/rd,rh->dh/dot_general | solution.py:110
  156.7 3.3 %fusion.15 = f32[6144,128]{1,0:T(8,128)S(1)} fusion(bf16[256,128]{1,0:T(8,128)(2,1)S(1)} %copy-done.7, bf16[2,256,6144]{2,1,0:T(8,128)(2,1)} %all-gather.2.cloned.1.call-done), kind=kOutput, calls=%fused_computation.28 | convolution fusion | flops 402653184 | bytes 6356992 | tf_op jit(solution)/shard_map/rd,rh->dh/dot_general | solution.py:114
  160.0 2.2 fusion.10
  162.2 2.2 fusion.11
  164.4 69.6 %reduce-scatter.2.cloned.1.call-done = bf16[384,512]{1,0:T(8,128)(2,1)} async-done(((bf16[6144,512]{1,0:T(8,128)(2,1)}), bf16[384,512]{1,0:T(8,128)(2,1)}) %reduce-scatter.2.cloned.1.call-update) | async-done | bytes 393232 | tf_op jit(solution)/shard_map/reduce_scatter | solution.py:104
  234.0 1.0 slice_bitcast_fusion.17
  236.2 5.8 %all-to-all-start.1 = ((bf16[8,64,384]{2,1,0:T(8,128)(2,1)}), bf16[8,64,384]{2,1,0:T(8,128)(2,1)S(1)}, u32[]{:S(2)}, u32[]{:S(2)}) async-start(bf16[8,64,384]{2,1,0:T(8,128)(2,1)} %pad_maximum_fusion.2), calls=%async_computation.2 | async-start | bytes 786432 | tf_op jit(solution)/shard_map/all_to_all | solution.py:129
  241.9 4.7 %fusion.9 = bf16[1,128,6144]{2,1,0:T(8,128)(2,1)} fusion(f32[128,6144]{1,0:T(8,128)} %fusion.12, bf16[256,128]{1,0:T(8,128)(2,1)S(1)} %get-tuple-element.12, bf16[2,256,6144]{2,1,0:T(8,128)(2,1)} %copy-done.2), kind=kOutput, calls=%fused_computation.17 | convolution fusion | flops 404226048 | bytes 7929856 | tf_op jit(solution)/shard_map/rh,rd->hd/dot_general | solution.py:119
  246.7 4.8 %all-to-all-done.1 = bf16[8,64,384]{2,1,0:T(8,128)(2,1)S(1)} async-done(((bf16[8,64,384]{2,1,0:T(8,128)(2,1)}), bf16[8,64,384]{2,1,0:T(8,128)(2,1)S(1)}, u32[]{:S(2)}, u32[]{:S(2)}) %all-to-all-start.1) | async-done | bytes 393248 | tf_op jit(solution)/shard_map/all_to_all | solution.py:129
  (67 shorter events, 14.2 us)
Async XLA Ops:
  7.2 116.4 %copy-start = (bf16[1,6144,128]{2,1,0:T(8,128)(2,1)S(1)}, bf16[1,6144,128]{2,1,0:T(8,128)(2,1)}, u32[]{:S(2)}) copy-start(bf16[1,6144,128]{2,1,0:T(8,128)(2,1)} %param.11) | copy-start | bytes 4718596
  7.2 113.7 %copy-start.3 = (bf16[1,128,6144]{2,1,0:T(8,128)(2,1)S(1)}, bf16[1,128,6144]{2,1,0:T(8,128)(2,1)}, u32[]{:S(2)}) copy-start(bf16[1,128,6144]{2,1,0:T(8,128)(2,1)} %param.12) | copy-start | bytes 4718596
  7.2 103.3 %all-gather.2.cloned.1.call-start = ((), (), s32[]{:S(2)}) async-start(), calls=%async_computation.3 | async-start | bytes 6684672 | tf_op jit(solution)/shard_map/all_gather | solution.py:59
  28.8 205.2 %reduce-scatter.2.cloned.1.call-start = ((), (), s32[]{:S(2)}) async-start(), calls=%async_computation.4 | async-start | bytes 6684672 | tf_op jit(solution)/shard_map/reduce_scatter | solution.py:104
  110.5 11.4 %copy-start.4 = (bf16[1,6144,128]{2,1,0:T(8,128)(2,1)S(1)}, bf16[1,6144,128]{2,1,0:T(8,128)(2,1)}, u32[]{:S(2)}) copy-start(bf16[1,6144,128]{2,1,0:T(8,128)(2,1)} %param.10) | copy-start | bytes 4718596
  110.5 10.4 %collective-permute-start = (bf16[2,256,6144]{2,1,0:T(8,128)(2,1)}, bf16[2,256,6144]{2,1,0:T(8,128)(2,1)S(1)}, u32[]{:S(2)}, u32[]{:S(2)}) collective-permute-start(bf16[2,256,6144]{2,1,0:T(8,128)(2,1)} %all-gather.2.cloned.1.call-done), channel_id=1, source_target_pairs={{0,16},{16,0},{1,17},{17,1},{2,18},{18,2},{3,19},{19,3},{4,20},{20... | collective-permute-start | bytes 18874376 | tf_op jit(solution)/shard_map/ppermute | solution.py:61
  120.9 2.7 %copy-start.2 = (bf16[2,256,6144]{2,1,0:T(8,128)(2,1)}, bf16[2,256,6144]{2,1,0:T(8,128)(2,1)S(1)}, u32[]{:S(2)}) copy-start(bf16[2,256,6144]{2,1,0:T(8,128)(2,1)S(1)} %collective-permute-done) | copy-start | bytes 18874372
  126.6 7.9 %slice-start.2 = ((s8[6291456]{0:T(1024)(128)(4,1)}), s8[4194304]{0:T(1024)(128)(4,1)S(1)}, s32[]{:S(2)}) async-start(s8[6291456]{0:T(1024)(128)(4,1)} %bitcast.108), calls=%async_computation.7 | async-start | bytes 8388608
  129.3 5.2 %slice-start.3 = ((s8[6291456]{0:T(1024)(128)(4,1)}), s8[2097152]{0:T(1024)(128)(4,1)S(1)}, s32[]{:S(2)}) async-start(s8[6291456]{0:T(1024)(128)(4,1)} %bitcast.108), calls=%async_computation.8 | async-start | bytes 4194304
  134.4 1.4 copy-start.5
  134.4 10.4 %collective-permute-start.1 = (bf16[6144,512]{1,0:T(8,128)(2,1)}, bf16[6144,512]{1,0:T(8,128)(2,1)S(1)}, u32[]{:S(2)}, u32[]{:S(2)}) collective-permute-start(bf16[6144,512]{1,0:T(8,128)(2,1)} %pad_maximum_fusion), channel_id=1, source_target_pairs={{0,16},{16,0},{1,17},{17,1},{2,18},{18,2},{3,19},{19,3},{4,20},{20... | collective-permute-start | bytes 18874376 | tf_op jit(solution)/shard_map/ppermute | solution.py:101
  137.7 2.0 copy-start.8
  137.7 2.0 copy-start.10
  137.7 2.0 copy-start.6
  148.5 0.8 copy-start.11
  149.3 4.2 %copy-start.9 = (bf16[256,128]{1,0:T(8,128)(2,1)S(1)}, bf16[256,128]{1,0:T(8,128)(2,1)}, u32[]{:S(2)}) copy-start(bf16[256,128]{1,0:T(8,128)(2,1)} %copy-done.8) | copy-start | bytes 196612
  153.6 3.1 %copy-start.7 = (bf16[256,128]{1,0:T(8,128)(2,1)S(1)}, bf16[256,128]{1,0:T(8,128)(2,1)}, u32[]{:S(2)}) copy-start(bf16[256,128]{1,0:T(8,128)(2,1)} %copy-done.6) | copy-start | bytes 196612
  153.6 6.4 %slice-start = ((s8[6291456]{0:T(1024)(128)(4,1)}), s8[4194304]{0:T(1024)(128)(4,1)S(1)}, s32[]{:S(2)}) async-start(s8[6291456]{0:T(1024)(128)(4,1)} %bitcast.106), calls=%async_computation.5 | async-start | bytes 8388608
  156.7 3.3 %slice-start.1 = ((s8[6291456]{0:T(1024)(128)(4,1)}), s8[2097152]{0:T(1024)(128)(4,1)S(1)}, s32[]{:S(2)}) async-start(s8[6291456]{0:T(1024)(128)(4,1)} %bitcast.106), calls=%async_computation.6 | async-start | bytes 4194304
  236.2 15.2 %all-to-all-start.1 = ((bf16[8,64,384]{2,1,0:T(8,128)(2,1)}), bf16[8,64,384]{2,1,0:T(8,128)(2,1)S(1)}, u32[]{:S(2)}, u32[]{:S(2)}) async-start(bf16[8,64,384]{2,1,0:T(8,128)(2,1)} %pad_maximum_fusion.2), calls=%async_computation.2 | async-start | bytes 786432 | tf_op jit(solution)/shard_map/all_to_all | solution.py:129
  241.9 11.4 %copy-start.1 = (bf16[1,6144,128]{2,1,0:T(8,128)(2,1)S(1)}, bf16[1,6144,128]{2,1,0:T(8,128)(2,1)}, u32[]{:S(2)}) copy-start(bf16[1,6144,128]{2,1,0:T(8,128)(2,1)} %param.11) | copy-start | bytes 4718596
Sparse Core Ops, SparseCore 0:
  28.9 81.5 all-gather.1
  148.6 85.3 reduce-scatter.1

commit v5 on v4

--- a/solution.py
+++ b/solution.py
@@ -76,7 +76,7 @@
         out_t = with_layout_constraint(out_t, Layout(major_to_minor=(0, 1)))
         return gate_pre, up_pre, sigmoid_gate, activated, hidden, out_t
 
-    def backward(rows, grads, gate_pre, up_pre, sigmoid_gate, activated):
+    def backward(grads, gate_pre, up_pre, sigmoid_gate, activated):
         hidden_grad = jnp.einsum(
             "rd,hd->rh", grads, down_local, preferred_element_type=jnp.float32
         )
@@ -94,10 +94,9 @@
     rows_a, grads_a = mine_full[0], mine_full[1]
     rows_b, grads_b = other_full[0], other_full[1]
     fa = forward(rows_a)
+    ga, ua, back_a = backward(grads_a, *fa[:4])
     fb = forward(rows_b)
-
-    ga, ua, back_a = backward(rows_a, grads_a, *fa[:4])
-    gb, ub, back_b = backward(rows_b, grads_b, *fb[:4])
+    gb, ub, back_b = backward(grads_b, *fb[:4])
     partner = lax.ppermute(jnp.concatenate([fb[5], back_b], axis=1), "core", pair)
     own = jnp.concatenate([fa[5], back_a], axis=1)
     summed = (own.astype(jnp.float32) + partner.astype(jnp.float32)).astype(jnp.bfloat16)

time: 261 us -> 261 us (level)
  no operation moved by 1% of the time
where the time goes in v5:
time: 261 us; the launch traced here: 260 us
  waiting for transfers between devices  170 us (65%)
  matrix products  37.1 us (14%)
  blocking collectives  16.1 us (6%)
  between operations  14.3 us (5%)
  other arithmetic  12 us (5%)
  starting transfers between devices  5.97 us (2%)
  local copies, waits for them, and re-layouts  4.14 us (2%)
    all_gather x1, waiting for transfers between devices, per_device(): mine_full = lax.all_gather(mine, TN, axis=2, tiled=True)  81.7 us
    reduce_scatter x1, waiting for transfers between devices, per_device(): scattered = lax.psum_scatter(summed, TN, scatter_dimension=0, tiled=True)  69.6 us
    all_to_all x1, blocking collectives, per_device(): recv = lax.all_to_all(send, SRC, split_axis=0, concat_axis=0, tiled=True)  16.1 us
    ppermute x1, waiting for transfers between devices, per_device(): other_full = lax.ppermute(mine_full, 'core', pair)  10.4 us
    all_to_all x1, starting transfers between devices, per_device(): lax.all_to_all(done, SRC, split_axis=0, concat_axis=0, tiled=True)  5.75 us
  transfers between devices with their start and end apart: 5, of which 5 were waited for; matrix products, arithmetic and copies ran while one was open for 10% of the time, Pallas kernels for 0%

profile of v5, /device:TPU:2, one launch (start us, length us, event | category | flops | bytes accessed | tf_op | source)
XLA Modules:
  0.0 260.2 jit_solution(12670048209112556618)
XLA Ops:
  10.8 1.1 convolution_convert_fusion.3
  11.9 16.1 %all_to_all.10 = bf16[8,64,384]{2,1,0:T(8,128)(2,1)S(1)} all-to-all(bf16[8,64,384]{2,1,0:T(8,128)(2,1)S(1)} %pad_maximum_fusion.1), channel_id=1, replica_groups=mesh['y'=4,'xhi'=2,'core'=2,'xlo'=2,'z'=8] {'y','xhi'}, dimensions={0} | all-to-all | bytes 786432 | tf_op jit(solution)/shard_map/all_to_all | solution.py:56
  28.9 81.7 %all-gather.2.cloned.1.call-done = bf16[2,256,6144]{2,1,0:T(8,128)(2,1)} async-done(((bf16[2,256,384]{2,1,0:T(8,128)(2,1)}), bf16[2,256,6144]{2,1,0:T(8,128)(2,1)}) %all-gather.2.cloned.1.call-update) | async-done | bytes 6291472 | tf_op jit(solution)/shard_map/all_gather | solution.py:59
  110.5 10.4 %collective-permute-done = bf16[2,256,6144]{2,1,0:T(8,128)(2,1)S(1)} collective-permute-done((bf16[2,256,6144]{2,1,0:T(8,128)(2,1)}, bf16[2,256,6144]{2,1,0:T(8,128)(2,1)S(1)}, u32[]{:S(2)}, u32[]{:S(2)}) %collective-permute-start) | collective-permute-done | bytes 6291488 | tf_op jit(solution)/shard_map/ppermute | solution.py:61
  120.9 1.0 fusion.14
  121.9 1.1 fusion.20
  123.6 1.0 multiply_convert_fusion.2
  124.6 1.0 fusion.3
  126.6 2.7 %fusion.4 = bf16[6144,256]{1,0:T(8,128)(2,1)} fusion(f32[256,6144]{0,1:T(8,128)S(1)} %fusion.29, bf16[256,128]{1,0:T(8,128)(2,1)S(1)} %get-tuple-element.14, bf16[1,6144,128]{2,1,0:T(8,128)(2,1)S(1)} %copy-done), kind=kOutput, calls=%fused_computation.12 | convolution fusion | flops 405798912 | bytes 11075584 | tf_op jit(solution)/shard_map/dh,rh->dr/dot_general | solution.py:89
  129.3 5.1 %pad_maximum_fusion = bf16[6144,512]{1,0:T(8,128)(2,1)} fusion(bf16[6144,256]{1,0:T(8,128)(2,1)} %fusion.4, bf16[6144,256]{1,0:T(8,128)(2,1)S(1)} %fusion.3), kind=kLoop, calls=%fused_computation.20 | loop fusion | flops 12582912 | bytes 12582912 | tf_op jit(solution)/shard_map/concatenate | solution.py:100
  137.8 1.0 fusion.2
  139.8 1.0 fusion.5
  140.8 4.0 %collective-permute-done.1 = bf16[6144,512]{1,0:T(8,128)(2,1)S(1)} collective-permute-done((bf16[6144,512]{1,0:T(8,128)(2,1)}, bf16[6144,512]{1,0:T(8,128)(2,1)S(1)}, u32[]{:S(2)}, u32[]{:S(2)}) %collective-permute-start.1) | collective-permute-done | bytes 6291488 | tf_op jit(solution)/shard_map/ppermute | solution.py:100
  144.7 3.8 %add_convert_fusion = bf16[6144,512]{1,0:T(8,128)(2,1)} fusion(bf16[6144,512]{1,0:T(8,128)(2,1)S(1)} %collective-permute-done.1, bf16[6144,256]{1,0:T(8,128)(2,1)S(1)} %fusion.5, bf16[6144,256]{1,0:T(8,128)(2,1)S(1)} %fusion.2), kind=kLoop, calls=%fused_computation | loop fusion | flops 22020096 | bytes 18874368 | tf_op jit(solution)/shard_map/convert_element_type | solution.py:102
  149.3 4.2 %fusion.12 = f32[128,6144]{1,0:T(8,128)} fusion(bf16[256,128]{1,0:T(8,128)(2,1)S(1)} %copy-done.11, bf16[2,256,6144]{2,1,0:T(8,128)(2,1)} %all-gather.2.cloned.1.call-done), kind=kOutput, calls=%fused_computation.25 | convolution fusion | flops 402653184 | bytes 6356992 | tf_op jit(solution)/shard_map/rh,rd->hd/dot_general | solution.py:117
  153.6 3.1 %fusion.16 = f32[6144,128]{1,0:T(8,128)S(1)} fusion(bf16[256,128]{1,0:T(8,128)(2,1)S(1)} %copy-done.9, bf16[2,256,6144]{2,1,0:T(8,128)(2,1)} %all-gather.2.cloned.1.call-done), kind=kOutput, calls=%fused_computation.29 | convolution fusion | flops 402653184 | bytes 6356992 | tf_op jit(solution)/shard_map/rd,rh->dh/dot_general | solution.py:109
  156.7 3.3 %fusion.15 = f32[6144,128]{1,0:T(8,128)S(1)} fusion(bf16[256,128]{1,0:T(8,128)(2,1)S(1)} %copy-done.7, bf16[2,256,6144]{2,1,0:T(8,128)(2,1)} %all-gather.2.cloned.1.call-done), kind=kOutput, calls=%fused_computation.28 | convolution fusion | flops 402653184 | bytes 6356992 | tf_op jit(solution)/shard_map/rd,rh->dh/dot_general | solution.py:113
  160.0 2.2 fusion.10
  162.2 2.2 fusion.11
  164.4 69.6 %reduce-scatter.2.cloned.1.call-done = bf16[384,512]{1,0:T(8,128)(2,1)} async-done(((bf16[6144,512]{1,0:T(8,128)(2,1)}), bf16[384,512]{1,0:T(8,128)(2,1)}) %reduce-scatter.2.cloned.1.call-update) | async-done | bytes 393232 | tf_op jit(solution)/shard_map/reduce_scatter | solution.py:103
  234.0 1.0 slice_bitcast_fusion.17
  236.2 5.8 %all-to-all-start.1 = ((bf16[8,64,384]{2,1,0:T(8,128)(2,1)}), bf16[8,64,384]{2,1,0:T(8,128)(2,1)S(1)}, u32[]{:S(2)}, u32[]{:S(2)}) async-start(bf16[8,64,384]{2,1,0:T(8,128)(2,1)} %pad_maximum_fusion.2), calls=%async_computation.2 | async-start | bytes 786432 | tf_op jit(solution)/shard_map/all_to_all | solution.py:128
  241.9 4.7 %fusion.9 = bf16[1,128,6144]{2,1,0:T(8,128)(2,1)} fusion(f32[128,6144]{1,0:T(8,128)} %fusion.12, bf16[256,128]{1,0:T(8,128)(2,1)S(1)} %get-tuple-element.12, bf16[2,256,6144]{2,1,0:T(8,128)(2,1)} %copy-done.2), kind=kOutput, calls=%fused_computation.17 | convolution fusion | flops 404226048 | bytes 7929856 | tf_op jit(solution)/shard_map/rh,rd->hd/dot_general | solution.py:118
  246.7 4.8 %all-to-all-done.1 = bf16[8,64,384]{2,1,0:T(8,128)(2,1)S(1)} async-done(((bf16[8,64,384]{2,1,0:T(8,128)(2,1)}), bf16[8,64,384]{2,1,0:T(8,128)(2,1)S(1)}, u32[]{:S(2)}, u32[]{:S(2)}) %all-to-all-start.1) | async-done | bytes 393248 | tf_op jit(solution)/shard_map/all_to_all | solution.py:128
  (67 shorter events, 14.2 us)
Async XLA Ops:
  7.2 116.4 %copy-start = (bf16[1,6144,128]{2,1,0:T(8,128)(2,1)S(1)}, bf16[1,6144,128]{2,1,0:T(8,128)(2,1)}, u32[]{:S(2)}) copy-start(bf16[1,6144,128]{2,1,0:T(8,128)(2,1)} %param.11) | copy-start | bytes 4718596
  7.2 113.7 %copy-start.3 = (bf16[1,128,6144]{2,1,0:T(8,128)(2,1)S(1)}, bf16[1,128,6144]{2,1,0:T(8,128)(2,1)}, u32[]{:S(2)}) copy-start(bf16[1,128,6144]{2,1,0:T(8,128)(2,1)} %param.12) | copy-start | bytes 4718596
  7.2 103.3 %all-gather.2.cloned.1.call-start = ((), (), s32[]{:S(2)}) async-start(), calls=%async_computation.3 | async-start | bytes 6684672 | tf_op jit(solution)/shard_map/all_gather | solution.py:59
  28.8 205.2 %reduce-scatter.2.cloned.1.call-start = ((), (), s32[]{:S(2)}) async-start(), calls=%async_computation.4 | async-start | bytes 6684672 | tf_op jit(solution)/shard_map/reduce_scatter | solution.py:103
  110.5 11.4 %copy-start.4 = (bf16[1,6144,128]{2,1,0:T(8,128)(2,1)S(1)}, bf16[1,6144,128]{2,1,0:T(8,128)(2,1)}, u32[]{:S(2)}) copy-start(bf16[1,6144,128]{2,1,0:T(8,128)(2,1)} %param.10) | copy-start | bytes 4718596
  110.5 10.4 %collective-permute-start = (bf16[2,256,6144]{2,1,0:T(8,128)(2,1)}, bf16[2,256,6144]{2,1,0:T(8,128)(2,1)S(1)}, u32[]{:S(2)}, u32[]{:S(2)}) collective-permute-start(bf16[2,256,6144]{2,1,0:T(8,128)(2,1)} %all-gather.2.cloned.1.call-done), channel_id=1, source_target_pairs={{0,16},{16,0},{1,17},{17,1},{2,18},{18,2},{3,19},{19,3},{4,20},{20... | collective-permute-start | bytes 18874376 | tf_op jit(solution)/shard_map/ppermute | solution.py:61
  120.9 2.7 %copy-start.2 = (bf16[2,256,6144]{2,1,0:T(8,128)(2,1)}, bf16[2,256,6144]{2,1,0:T(8,128)(2,1)S(1)}, u32[]{:S(2)}) copy-start(bf16[2,256,6144]{2,1,0:T(8,128)(2,1)S(1)} %collective-permute-done) | copy-start | bytes 18874372
  126.6 7.9 %slice-start.2 = ((s8[6291456]{0:T(1024)(128)(4,1)}), s8[4194304]{0:T(1024)(128)(4,1)S(1)}, s32[]{:S(2)}) async-start(s8[6291456]{0:T(1024)(128)(4,1)} %bitcast.108), calls=%async_computation.7 | async-start | bytes 8388608
  129.3 5.2 %slice-start.3 = ((s8[6291456]{0:T(1024)(128)(4,1)}), s8[2097152]{0:T(1024)(128)(4,1)S(1)}, s32[]{:S(2)}) async-start(s8[6291456]{0:T(1024)(128)(4,1)} %bitcast.108), calls=%async_computation.8 | async-start | bytes 4194304
  134.4 1.4 copy-start.5
  134.4 10.4 %collective-permute-start.1 = (bf16[6144,512]{1,0:T(8,128)(2,1)}, bf16[6144,512]{1,0:T(8,128)(2,1)S(1)}, u32[]{:S(2)}, u32[]{:S(2)}) collective-permute-start(bf16[6144,512]{1,0:T(8,128)(2,1)} %pad_maximum_fusion), channel_id=1, source_target_pairs={{0,16},{16,0},{1,17},{17,1},{2,18},{18,2},{3,19},{19,3},{4,20},{20... | collective-permute-start | bytes 18874376 | tf_op jit(solution)/shard_map/ppermute | solution.py:100
  137.7 2.0 copy-start.8
  137.7 2.0 copy-start.10
  137.7 2.0 copy-start.6
  148.5 0.8 copy-start.11
  149.3 4.2 %copy-start.9 = (bf16[256,128]{1,0:T(8,128)(2,1)S(1)}, bf16[256,128]{1,0:T(8,128)(2,1)}, u32[]{:S(2)}) copy-start(bf16[256,128]{1,0:T(8,128)(2,1)} %copy-done.8) | copy-start | bytes 196612
  153.6 3.1 %copy-start.7 = (bf16[256,128]{1,0:T(8,128)(2,1)S(1)}, bf16[256,128]{1,0:T(8,128)(2,1)}, u32[]{:S(2)}) copy-start(bf16[256,128]{1,0:T(8,128)(2,1)} %copy-done.6) | copy-start | bytes 196612
  153.6 6.4 %slice-start = ((s8[6291456]{0:T(1024)(128)(4,1)}), s8[4194304]{0:T(1024)(128)(4,1)S(1)}, s32[]{:S(2)}) async-start(s8[6291456]{0:T(1024)(128)(4,1)} %bitcast.106), calls=%async_computation.5 | async-start | bytes 8388608
  156.7 3.3 %slice-start.1 = ((s8[6291456]{0:T(1024)(128)(4,1)}), s8[2097152]{0:T(1024)(128)(4,1)S(1)}, s32[]{:S(2)}) async-start(s8[6291456]{0:T(1024)(128)(4,1)} %bitcast.106), calls=%async_computation.6 | async-start | bytes 4194304
  236.2 15.2 %all-to-all-start.1 = ((bf16[8,64,384]{2,1,0:T(8,128)(2,1)}), bf16[8,64,384]{2,1,0:T(8,128)(2,1)S(1)}, u32[]{:S(2)}, u32[]{:S(2)}) async-start(bf16[8,64,384]{2,1,0:T(8,128)(2,1)} %pad_maximum_fusion.2), calls=%async_computation.2 | async-start | bytes 786432 | tf_op jit(solution)/shard_map/all_to_all | solution.py:128
  241.9 11.4 %copy-start.1 = (bf16[1,6144,128]{2,1,0:T(8,128)(2,1)S(1)}, bf16[1,6144,128]{2,1,0:T(8,128)(2,1)}, u32[]{:S(2)}) copy-start(bf16[1,6144,128]{2,1,0:T(8,128)(2,1)} %param.11) | copy-start | bytes 4718596
Sparse Core Ops, SparseCore 0:
  28.9 81.5 all-gather.1
  148.6 85.3 reduce-scatter.1

commit v6 on v5

--- a/solution.py
+++ b/solution.py
@@ -58,65 +58,68 @@
     mine = mine.reshape(2, n_src * CAP, feature_cols)
     mine_full = lax.all_gather(mine, TN, axis=2, tiled=True)
     pair = [(0, 1), (1, 0)]
-    other_full = lax.ppermute(mine_full, "core", pair)
 
     gate_local = gate_matrix[0]
     up_local = up_matrix[0]
     down_local = down_matrix[0]
+    gate_other, up_other, down_other = lax.ppermute(
+        (gate_local, up_local, down_local), "core", pair
+    )
 
-    def forward(rows):
-        gate_pre = jnp.dot(rows, gate_local, preferred_element_type=jnp.float32)
-        up_pre = jnp.dot(rows, up_local, preferred_element_type=jnp.float32)
+    def forward(rows, gate_w, up_w, down_w):
+        gate_pre = jnp.dot(rows, gate_w, preferred_element_type=jnp.float32)
+        up_pre = jnp.dot(rows, up_w, preferred_element_type=jnp.float32)
         sigmoid_gate = jax.nn.sigmoid(gate_pre)
         activated = gate_pre * sigmoid_gate
         hidden = (activated * up_pre).astype(jnp.bfloat16)
         out_t = jnp.einsum(
-            "hd,rh->dr", down_local, hidden, preferred_element_type=jnp.float32
+            "hd,rh->dr", down_w, hidden, preferred_element_type=jnp.float32
         ).astype(jnp.bfloat16)
         out_t = with_layout_constraint(out_t, Layout(major_to_minor=(0, 1)))
         return gate_pre, up_pre, sigmoid_gate, activated, hidden, out_t
 
-    def backward(grads, gate_pre, up_pre, sigmoid_gate, activated):
+    def backward(grads, gate_pre, up_pre, sigmoid_gate, activated, gate_w, up_w, down_w):
         hidden_grad = jnp.einsum(
-            "rd,hd->rh", grads, down_local, preferred_element_type=jnp.float32
+            "rd,hd->rh", grads, down_w, preferred_element_type=jnp.float32
         )
         gate_grad = (
             hidden_grad * up_pre * sigmoid_gate * (1.0 + gate_pre * (1.0 - sigmoid_gate))
         ).astype(jnp.bfloat16)
         up_grad = (hidden_grad * activated).astype(jnp.bfloat16)
         back_t = (
-            jnp.einsum("dh,rh->dr", gate_local, gate_grad, preferred_element_type=jnp.float32)
-            + jnp.einsum("dh,rh->dr", up_local, up_grad, preferred_element_type=jnp.float32)
+            jnp.einsum("dh,rh->dr", gate_w, gate_grad, preferred_element_type=jnp.float32)
+            + jnp.einsum("dh,rh->dr", up_w, up_grad, preferred_element_type=jnp.float32)
         ).astype(jnp.bfloat16)
         back_t = with_layout_constraint(back_t, Layout(major_to_minor=(0, 1)))
         return gate_grad, up_grad, back_t
 
-    rows_a, grads_a = mine_full[0], mine_full[1]
-    rows_b, grads_b = other_full[0], other_full[1]
-    fa = forward(rows_a)
-    ga, ua, back_a = backward(grads_a, *fa[:4])
-    fb = forward(rows_b)
-    gb, ub, back_b = backward(grads_b, *fb[:4])
-    partner = lax.ppermute(jnp.concatenate([fb[5], back_b], axis=1), "core", pair)
-    own = jnp.concatenate([fa[5], back_a], axis=1)
-    summed = (own.astype(jnp.float32) + partner.astype(jnp.float32)).astype(jnp.bfloat16)
+    rows, grads = mine_full[0], mine_full[1]
+    own_w = (gate_local, up_local, down_local)
+    other_w = (gate_other, up_other, down_other)
+    f_own = forward(rows, *own_w)
+    f_other = forward(rows, *other_w)
+    b_own = backward(grads, *f_own[:4], *own_w)
+    b_other = backward(grads, *f_other[:4], *other_w)
+    own = jnp.concatenate([f_own[5], b_own[2]], axis=1)
+    other = jnp.concatenate([f_other[5], b_other[2]], axis=1)
+    summed = (own.astype(jnp.float32) + other.astype(jnp.float32)).astype(jnp.bfloat16)
     scattered = lax.psum_scatter(summed, TN, scatter_dimension=0, tiled=True)
-    n_rows = fa[5].shape[1]
+    n_rows = f_own[5].shape[1]
     out_rows = scattered[:, :n_rows].T
     back_rows = scattered[:, n_rows:].T
 
-    gate_gradient = (
-        jnp.einsum("rd,rh->dh", rows_a, ga, preferred_element_type=jnp.float32)
-        + jnp.einsum("rd,rh->dh", rows_b, gb, preferred_element_type=jnp.float32)
-    ).astype(jnp.bfloat16)[None]
-    up_gradient = (
-        jnp.einsum("rd,rh->dh", rows_a, ua, preferred_element_type=jnp.float32)
-        + jnp.einsum("rd,rh->dh", rows_b, ub, preferred_element_type=jnp.float32)
-    ).astype(jnp.bfloat16)[None]
-    down_gradient = (
-        jnp.einsum("rh,rd->hd", fa[4], grads_a, preferred_element_type=jnp.float32)
-        + jnp.einsum("rh,rd->hd", fb[4], grads_b, preferred_element_type=jnp.float32)
-    ).astype(jnp.bfloat16)[None]
+    def weight_grads(f, b):
+        return (
+            jnp.einsum("rd,rh->dh", rows, b[0], preferred_element_type=jnp.float32),
+            jnp.einsum("rd,rh->dh", rows, b[1], preferred_element_type=jnp.float32),
+            jnp.einsum("rh,rd->hd", f[4], grads, preferred_element_type=jnp.float32),
+        )
+
+    w_own = weight_grads(f_own, b_own)
+    w_recv = lax.ppermute(weight_grads(f_other, b_other), "core", pair)
+    gate_gradient = (w_own[0] + w_recv[0]).astype(jnp.bfloat16)[None]
+    up_gradient = (w_own[1] + w_recv[1]).astype(jnp.bfloat16)[None]
+    down_gradient = (w_own[2] + w_recv[2]).astype(jnp.bfloat16)[None]
 
     done = jnp.concatenate(
         [

time: 261 us -> 249 us (0.954)
  waiting for transfers between devices: 170 us -> 159 us
  other arithmetic: 12 us -> 7.26 us
  matrix products: 37.1 us -> 40.7 us
    ppermute x2 -> x6, waiting for transfers between devices: 14.3 us -> 3.91 us  [the longest x3 3.9 us: per_device(): w_recv = lax.ppermute(weight_grads(f_other, b_other), 'core', pair)]
    concatenate x1 -> x0, other arithmetic: 5.08 us -> none  [per_device(): jnp.concatenate([fb[5], back_b], axis=1)]
    dot_general x18, matrix products: 33.3 us -> 37.6 us  [the longest x2 6.86 us: weight_grads(): jnp.einsum('rh,rd->hd', f[4], grads, preferred_element_type=jnp.float32)]
  transfers between devices with their start and end apart: 5 -> 9, of which waited for: 5 -> 5; matrix products, arithmetic and copies ran while one was open for 10% -> 13% of each run, Pallas kernels for 0% -> 0%
where the time goes in v6:
time: 249 us
  waiting for transfers between devices  159 us (64%)
  matrix products  40.7 us (16%)
  blocking collectives  16.1 us (6%)
  between operations  14.4 us (6%)
  starting transfers between devices  7.74 us (3%)
  other arithmetic  7.26 us (3%)
  local copies, waits for them, and re-layouts  3.77 us (2%)
    all_gather x1, waiting for transfers between devices, per_device(): mine_full = lax.all_gather(mine, TN, axis=2, tiled=True)  81 us
    reduce_scatter x1, waiting for transfers between devices, per_device(): scattered = lax.psum_scatter(summed, TN, scatter_dimension=0, tiled=True)  68.8 us
    all_to_all x1, blocking collectives, per_device(): recv = lax.all_to_all(send, SRC, split_axis=0, concat_axis=0, tiled=True)  16.1 us
    dot_general x2, matrix products, weight_grads(): jnp.einsum('rh,rd->hd', f[4], grads, preferred_element_type=jnp.float32)  6.86 us
    all_to_all x1, starting transfers between devices, per_device(): lax.all_to_all(done, SRC, split_axis=0, concat_axis=0, tiled=True)  6.28 us
    dot_general x2, matrix products, forward(): gate_pre = jnp.dot(rows, gate_w, preferred_element_type=jnp.float32)  5.88 us
    dot_general x2, matrix products, weight_grads(): jnp.einsum('rd,rh->dh', rows, b[1], preferred_element_type=jnp.float32)  5.33 us
  transfers between devices with their start and end apart: 9, of which 5 were waited for; matrix products, arithmetic and copies ran while one was open for 13% of the time, Pallas kernels for 0%

profile of v6, /device:TPU:2, one launch (start us, length us, event | category | flops | bytes accessed | tf_op | source)
XLA Modules:
  0.0 248.5 jit_solution(6225838910146332056)
XLA Ops:
  11.1 16.1 %all_to_all.10 = bf16[8,64,384]{2,1,0:T(8,128)(2,1)S(1)} all-to-all(bf16[8,64,384]{2,1,0:T(8,128)(2,1)S(1)} %pad_maximum_fusion), channel_id=1, replica_groups=mesh['y'=4,'xhi'=2,'core'=2,'xlo'=2,'z'=8] {'y','xhi'}, dimensions={0} | all-to-all | bytes 786432 | tf_op jit(solution)/shard_map/all_to_all | solution.py:56
  28.7 81.0 %all-gather.2.cloned.1.call-done = bf16[2,256,6144]{2,1,0:T(8,128)(2,1)} async-done(((bf16[2,256,384]{2,1,0:T(8,128)(2,1)}), bf16[2,256,6144]{2,1,0:T(8,128)(2,1)}) %all-gather.2.cloned.1.call-update) | async-done | bytes 6291472 | tf_op jit(solution)/shard_map/all_gather | solution.py:59
  109.7 3.0 %fusion.14 = f32[256,128]{1,0:T(8,128)S(1)} fusion(bf16[2,256,6144]{2,1,0:T(8,128)(2,1)} %all-gather.2.cloned.1.call-done, bf16[1,128,6144]{2,1,0:T(8,128)(2,1)S(1)} %copy-done.3), kind=kOutput, calls=%fused_computation.24 | convolution fusion | flops 402653184 | bytes 4849664 | tf_op jit(solution)/shard_map/rd,hd->rh/dot_general | solution.py:82
  112.7 3.4 %fusion.20 = f32[256,128]{1,0:T(8,128)S(1)} fusion(bf16[2,256,6144]{2,1,0:T(8,128)(2,1)} %all-gather.2.cloned.1.call-done, bf16[1,6144,128]{2,1,0:T(8,128)(2,1)} %param.10), kind=kOutput, calls=%fused_computation.34 | convolution fusion | flops 402653184 | bytes 4849664 | tf_op jit(solution)/shard_map/dot_general | solution.py:70
  116.1 1.0 fusion.13
  118.5 1.0 fusion.2
  119.6 2.5 %fusion.18 = f32[256,128]{1,0:T(8,128)S(1)} fusion(bf16[6144,128]{1,0:T(8,128)(2,1)} %collective-permute-done, bf16[2,256,6144]{2,1,0:T(8,128)(2,1)S(1)} %copy-done.2), kind=kOutput, calls=%fused_computation.32 | convolution fusion | flops 402653184 | bytes 4849664 | tf_op jit(solution)/shard_map/dot_general | solution.py:70
  124.1 2.4 multiply_convert_fusion.2
  126.5 2.4 fusion.35
  129.0 1.0 fusion.3
  130.0 2.4 fusion.4
  132.5 4.1 %add_convert_fusion = bf16[6144,512]{1,0:T(8,128)(2,1)} fusion(bf16[6144,256]{1,0:T(8,128)(2,1)S(1)} %fusion.5, bf16[6144,256]{1,0:T(8,128)(2,1)S(1)} %fusion.2, bf16[6144,256]{1,0:T(8,128)(2,1)S(1)} %fusion.4, bf16[6144,256]{1,0:T(8,128)(2,1)S(1)} %fusion.3), kind=kLoop, calls=%fused_computation | loop fusion | flops 31457280 | bytes 18874368 | tf_op jit(solution)/shard_map/convert_element_type | solution.py:105
  137.4 3.1 %fusion.15 = f32[6144,128]{1,0:T(8,128)S(1)} fusion(bf16[256,128]{1,0:T(8,128)(2,1)S(1)} %copy-done.13, bf16[2,256,6144]{2,1,0:T(8,128)(2,1)} %all-gather.2.cloned.1.call-done), kind=kOutput, calls=%fused_computation.29 | convolution fusion | flops 402653184 | bytes 6356992 | tf_op jit(solution)/shard_map/rd,rh->dh/dot_general | solution.py:114
  140.7 1.0 fusion.16
  142.3 2.3 fusion.12
  144.6 1.7 collective-permute-done.4
  146.3 2.2 fusion.10
  148.5 2.2 collective-permute-done.3
  150.8 2.2 fusion.11
  153.0 68.8 %reduce-scatter.2.cloned.1.call-done = bf16[384,512]{1,0:T(8,128)(2,1)} async-done(((bf16[6144,512]{1,0:T(8,128)(2,1)}), bf16[384,512]{1,0:T(8,128)(2,1)}) %reduce-scatter.2.cloned.1.call-update) | async-done | bytes 393232 | tf_op jit(solution)/shard_map/reduce_scatter | solution.py:106
  221.8 1.0 slice_bitcast_fusion.15
  224.0 6.3 %all-to-all-start.1 = ((bf16[8,64,384]{2,1,0:T(8,128)(2,1)}), bf16[8,64,384]{2,1,0:T(8,128)(2,1)S(1)}, u32[]{:S(2)}, u32[]{:S(2)}) async-start(bf16[8,64,384]{2,1,0:T(8,128)(2,1)} %pad_maximum_fusion.1), calls=%async_computation.2 | async-start | bytes 786432 | tf_op jit(solution)/shard_map/all_to_all | solution.py:131
  230.3 4.6 %fusion.9 = bf16[1,128,6144]{2,1,0:T(8,128)(2,1)} fusion(f32[128,6144]{1,0:T(8,128)} %collective-permute-done.5, bf16[256,128]{1,0:T(8,128)(2,1)S(1)} %get-tuple-element.12, bf16[2,256,6144]{2,1,0:T(8,128)(2,1)} %all-gather.2.cloned.1.call-done), kind=kOutput, calls=%fused_computation.17 | convolution fusion | flops 404226048 | bytes 7929856 | tf_op jit(solution)/shard_map/rh,rd->hd/dot_general | solution.py:115
  234.9 4.9 %all-to-all-done.1 = bf16[8,64,384]{2,1,0:T(8,128)(2,1)S(1)} async-done(((bf16[8,64,384]{2,1,0:T(8,128)(2,1)}), bf16[8,64,384]{2,1,0:T(8,128)(2,1)S(1)}, u32[]{:S(2)}, u32[]{:S(2)}) %all-to-all-start.1) | async-done | bytes 393248 | tf_op jit(solution)/shard_map/all_to_all | solution.py:131
  (73 shorter events, 13.3 us)
Async XLA Ops:
  7.2 2.6 %copy-start = (bf16[48,384]{1,0:T(8,128)(2,1)S(1)}, bf16[48,384]{1,0:T(8,128)(2,1)}, u32[]{:S(2)}) copy-start(bf16[48,384]{1,0:T(8,128)(2,1)} %param.13) | copy-start | bytes 110596
  7.2 20.9 %copy-start.3 = (bf16[1,128,6144]{2,1,0:T(8,128)(2,1)S(1)}, bf16[1,128,6144]{2,1,0:T(8,128)(2,1)}, u32[]{:S(2)}) copy-start(bf16[1,128,6144]{2,1,0:T(8,128)(2,1)} %param.12) | copy-start | bytes 4718596
  7.2 102.5 %all-gather.2.cloned.1.call-start = ((), (), s32[]{:S(2)}) async-start(), calls=%async_computation.3 | async-start | bytes 6684672 | tf_op jit(solution)/shard_map/all_gather | solution.py:59
  28.0 193.8 %reduce-scatter.2.cloned.1.call-start = ((), (), s32[]{:S(2)}) async-start(), calls=%async_computation.4 | async-start | bytes 6684672 | tf_op jit(solution)/shard_map/reduce_scatter | solution.py:106
  28.0 88.1 %collective-permute-start.2 = (bf16[128,6144]{1,0:T(8,128)(2,1)S(1)}, bf16[128,6144]{1,0:T(8,128)(2,1)S(1)}, u32[]{:S(2)}, u32[]{:S(2)}) collective-permute-start(bf16[128,6144]{1,0:T(8,128)(2,1)S(1)} %bitcast.98), channel_id=1, source_target_pairs={{0,16},{16,0},{1,17},{17,1},{2,18},{18,2},{3,19},{19,3},{4,20},{20... | collective-permute-start | bytes 4718600 | tf_op jit(solution)/shard_map/ppermute | solution.py:65
  28.1 91.4 %collective-permute-start = (bf16[6144,128]{1,0:T(8,128)(2,1)}, bf16[6144,128]{1,0:T(8,128)(2,1)}, u32[]{:S(2)}, u32[]{:S(2)}) collective-permute-start(bf16[6144,128]{1,0:T(8,128)(2,1)} %bitcast.99), channel_id=1, source_target_pairs={{0,16},{16,0},{1,17},{17,1},{2,18},{18,2},{3,19},{19,3},{4,20},{20... | collective-permute-start | bytes 4718600 | tf_op jit(solution)/shard_map/ppermute | solution.py:65
  28.6 95.4 %collective-permute-start.1 = (bf16[6144,128]{1,0:T(8,128)(2,1)}, bf16[6144,128]{1,0:T(8,128)(2,1)}, u32[]{:S(2)}, u32[]{:S(2)}) collective-permute-start(bf16[6144,128]{1,0:T(8,128)(2,1)} %bitcast.100), channel_id=1, source_target_pairs={{0,16},{16,0},{1,17},{17,1},{2,18},{18,2},{3,19},{19,3},{4,20},{20... | collective-permute-start | bytes 4718600 | tf_op jit(solution)/shard_map/ppermute | solution.py:65
  109.7 6.4 %copy-start.2 = (bf16[2,256,6144]{2,1,0:T(8,128)(2,1)S(1)}, bf16[2,256,6144]{2,1,0:T(8,128)(2,1)}, u32[]{:S(2)}) copy-start(bf16[2,256,6144]{2,1,0:T(8,128)(2,1)} %all-gather.2.cloned.1.call-done) | copy-start | bytes 18874372
  116.1 1.4 copy-start.5
  118.5 4.6 %copy-start.6 = (bf16[256,128]{1,0:T(8,128)(2,1)}, bf16[256,128]{1,0:T(8,128)(2,1)S(1)}, u32[]{:S(2)}) copy-start(bf16[256,128]{1,0:T(8,128)(2,1)S(1)} %get-tuple-element.14) | copy-start | bytes 196612
  119.5 2.6 %copy-start.4 = (bf16[1,6144,128]{2,1,0:T(8,128)(2,1)S(1)}, bf16[1,6144,128]{2,1,0:T(8,128)(2,1)}, u32[]{:S(2)}) copy-start(bf16[1,6144,128]{2,1,0:T(8,128)(2,1)} %param.10) | copy-start | bytes 4718596
  126.5 2.5 %copy-start.12 = (bf16[256,128]{1,0:T(8,128)(2,1)}, bf16[256,128]{1,0:T(8,128)(2,1)S(1)}, u32[]{:S(2)}) copy-start(bf16[256,128]{1,0:T(8,128)(2,1)S(1)} %get-tuple-element.11) | copy-start | bytes 196612
  126.5 2.5 copy-start.8
  126.5 3.5 %copy-start.10 = (bf16[256,128]{1,0:T(8,128)(2,1)}, bf16[256,128]{1,0:T(8,128)(2,1)S(1)}, u32[]{:S(2)}) copy-start(bf16[256,128]{1,0:T(8,128)(2,1)S(1)} %get-tuple-element.10) | copy-start | bytes 196612
  136.6 4.0 %slice-start = ((s8[6291456]{0:T(1024)(128)(4,1)}), s8[2097152]{0:T(1024)(128)(4,1)S(1)}, s32[]{:S(2)}) async-start(s8[6291456]{0:T(1024)(128)(4,1)} %bitcast.94), calls=%async_computation.5 | async-start | bytes 4194304
  137.4 3.3 %slice-start.1 = ((s8[6291456]{0:T(1024)(128)(4,1)}), s8[4194304]{0:T(1024)(128)(4,1)S(1)}, s32[]{:S(2)}) async-start(s8[6291456]{0:T(1024)(128)(4,1)} %bitcast.94), calls=%async_computation.6 | async-start | bytes 8388608
  137.4 3.3 %copy-start.11 = (bf16[256,128]{1,0:T(8,128)(2,1)S(1)}, bf16[256,128]{1,0:T(8,128)(2,1)}, u32[]{:S(2)}) copy-start(bf16[256,128]{1,0:T(8,128)(2,1)} %copy-done.10) | copy-start | bytes 196612
  140.5 1.8 copy-start.9
  140.5 5.7 %collective-permute-start.4 = (f32[6144,128]{1,0:T(8,128)S(1)}, f32[6144,128]{1,0:T(8,128)S(1)}, u32[]{:S(2)}, u32[]{:S(2)}) collective-permute-start(f32[6144,128]{1,0:T(8,128)S(1)} %fusion.15), channel_id=1, source_target_pairs={{0,16},{16,0},{1,17},{17,1},{2,18},{18,2},{3,19},{19,3},{4,20},{20... | collective-permute-start | bytes 9437192 | tf_op jit(solution)/shard_map/ppermute | solution.py:119
  141.8 4.5 %copy-start.7 = (bf16[256,128]{1,0:T(8,128)(2,1)S(1)}, bf16[256,128]{1,0:T(8,128)(2,1)}, u32[]{:S(2)}) copy-start(bf16[256,128]{1,0:T(8,128)(2,1)} %copy-done.6) | copy-start | bytes 196612
  141.8 9.0 %collective-permute-start.3 = (f32[6144,128]{1,0:T(8,128)S(1)}, f32[6144,128]{1,0:T(8,128)S(1)}, u32[]{:S(2)}, u32[]{:S(2)}) collective-permute-start(f32[6144,128]{1,0:T(8,128)S(1)} %fusion.16), channel_id=1, source_target_pairs={{0,16},{16,0},{1,17},{17,1},{2,18},{18,2},{3,19},{19,3},{4,20},{20... | collective-permute-start | bytes 9437192 | tf_op jit(solution)/shard_map/ppermute | solution.py:119
  144.5 85.8 %collective-permute-start.5 = (f32[128,6144]{1,0:T(8,128)}, f32[128,6144]{1,0:T(8,128)}, u32[]{:S(2)}, u32[]{:S(2)}) collective-permute-start(f32[128,6144]{1,0:T(8,128)} %fusion.12), channel_id=1, source_target_pairs={{0,16},{16,0},{1,17},{17,1},{2,18},{18,2},{3,19},{19,3},{4,20},{20... | collective-permute-start | bytes 9437192 | tf_op jit(solution)/shard_map/ppermute | solution.py:119
  224.0 15.8 %all-to-all-start.1 = ((bf16[8,64,384]{2,1,0:T(8,128)(2,1)}), bf16[8,64,384]{2,1,0:T(8,128)(2,1)S(1)}, u32[]{:S(2)}, u32[]{:S(2)}) async-start(bf16[8,64,384]{2,1,0:T(8,128)(2,1)} %pad_maximum_fusion.1), calls=%async_computation.2 | async-start | bytes 786432 | tf_op jit(solution)/shard_map/all_to_all | solution.py:131
  230.3 11.4 %copy-start.1 = (bf16[48,384]{1,0:T(8,128)(2,1)S(1)}, bf16[48,384]{1,0:T(8,128)(2,1)}, u32[]{:S(2)}) copy-start(bf16[48,384]{1,0:T(8,128)(2,1)} %param.13) | copy-start | bytes 110596
  (1 other events, 0.8 us)
Sparse Core Ops, SparseCore 0:
  28.1 81.5 all-gather.1
  136.7 85.0 reduce-scatter.1

commit v7 on v6

--- a/solution.py
+++ b/solution.py
@@ -62,13 +62,13 @@
     gate_local = gate_matrix[0]
     up_local = up_matrix[0]
     down_local = down_matrix[0]
-    gate_other, up_other, down_other = lax.ppermute(
-        (gate_local, up_local, down_local), "core", pair
-    )
+    gu_local = jnp.concatenate([gate_local, up_local], axis=1)
+    gu_other, down_other = lax.ppermute((gu_local, down_local), "core", pair)
 
-    def forward(rows, gate_w, up_w, down_w):
-        gate_pre = jnp.dot(rows, gate_w, preferred_element_type=jnp.float32)
-        up_pre = jnp.dot(rows, up_w, preferred_element_type=jnp.float32)
+    def forward(rows, gu_w, down_w):
+        pre = jnp.dot(rows, gu_w, preferred_element_type=jnp.float32)
+        width = pre.shape[1] // 2
+        gate_pre, up_pre = pre[:, :width], pre[:, width:]
         sigmoid_gate = jax.nn.sigmoid(gate_pre)
         activated = gate_pre * sigmoid_gate
         hidden = (activated * up_pre).astype(jnp.bfloat16)
@@ -78,7 +78,7 @@
         out_t = with_layout_constraint(out_t, Layout(major_to_minor=(0, 1)))
         return gate_pre, up_pre, sigmoid_gate, activated, hidden, out_t
 
-    def backward(grads, gate_pre, up_pre, sigmoid_gate, activated, gate_w, up_w, down_w):
+    def backward(grads, gate_pre, up_pre, sigmoid_gate, activated, gu_w, down_w):
         hidden_grad = jnp.einsum(
             "rd,hd->rh", grads, down_w, preferred_element_type=jnp.float32
         )
@@ -86,16 +86,16 @@
             hidden_grad * up_pre * sigmoid_gate * (1.0 + gate_pre * (1.0 - sigmoid_gate))
         ).astype(jnp.bfloat16)
         up_grad = (hidden_grad * activated).astype(jnp.bfloat16)
-        back_t = (
-            jnp.einsum("dh,rh->dr", gate_w, gate_grad, preferred_element_type=jnp.float32)
-            + jnp.einsum("dh,rh->dr", up_w, up_grad, preferred_element_type=jnp.float32)
+        both_grad = jnp.concatenate([gate_grad, up_grad], axis=1)
+        back_t = jnp.einsum(
+            "dh,rh->dr", gu_w, both_grad, preferred_element_type=jnp.float32
         ).astype(jnp.bfloat16)
         back_t = with_layout_constraint(back_t, Layout(major_to_minor=(0, 1)))
         return gate_grad, up_grad, back_t
 
     rows, grads = mine_full[0], mine_full[1]
-    own_w = (gate_local, up_local, down_local)
-    other_w = (gate_other, up_other, down_other)
+    own_w = (gu_local, down_local)
+    other_w = (gu_other, down_other)
     f_own = forward(rows, *own_w)
     f_other = forward(rows, *other_w)
     b_own = backward(grads, *f_own[:4], *own_w)

time: 249 us -> 244 us (0.980)
  matrix products: 40.7 us -> 36.5 us
  waiting for transfers between devices: 159 us -> 156 us
    dot_general x8 -> x4, matrix products: 16.1 us -> 7.68 us  [the longest x2 5.71 us: forward(): pre = jnp.dot(rows, gu_w, preferred_element_type=jnp.float32)]
    dot_general x2, matrix products: 2.05 us -> 4.92 us  [forward(): jnp.einsum('hd,rh->dr', down_w, hidden, preferred_element_type=jnp.float32)]
  transfers between devices with their start and end apart: 9 -> 8, of which waited for: 5 -> 5; matrix products, arithmetic and copies ran while one was open for 13% -> 13% of each run, Pallas kernels for 0% -> 0%
where the time goes in v7:
time: 244 us
  waiting for transfers between devices  156 us (64%)
  matrix products  36.5 us (15%)
  blocking collectives  16.1 us (7%)
  between operations  14.4 us (6%)
  other arithmetic  9.11 us (4%)
  starting transfers between devices  7.96 us (3%)
  local copies, waits for them, and re-layouts  3.72 us (2%)
    all_gather x1, waiting for transfers between devices, per_device(): mine_full = lax.all_gather(mine, TN, axis=2, tiled=True)  79.1 us
    reduce_scatter x1, waiting for transfers between devices, per_device(): scattered = lax.psum_scatter(summed, TN, scatter_dimension=0, tiled=True)  68.6 us
    all_to_all x1, blocking collectives, per_device(): recv = lax.all_to_all(send, SRC, split_axis=0, concat_axis=0, tiled=True)  16.1 us
    dot_general x2, matrix products, weight_grads(): jnp.einsum('rh,rd->hd', f[4], grads, preferred_element_type=jnp.float32)  6.87 us
    all_to_all x1, starting transfers between devices, per_device(): lax.all_to_all(done, SRC, split_axis=0, concat_axis=0, tiled=True)  6.46 us
    dot_general x2, matrix products, forward(): pre = jnp.dot(rows, gu_w, preferred_element_type=jnp.float32)  5.71 us
    dot_general x2, matrix products, backward(): jnp.einsum('rd,hd->rh', grads, down_w, preferred_element_type=jnp.float32)  5.34 us
    dot_general x2, matrix products, weight_grads(): jnp.einsum('rd,rh->dh', rows, b[1], preferred_element_type=jnp.float32)  5.32 us
  transfers between devices with their start and end apart: 8, of which 5 were waited for; matrix products, arithmetic and copies ran while one was open for 13% of the time, Pallas kernels for 0%

profile of v7, /device:TPU:2, one launch (start us, length us, event | category | flops | bytes accessed | tf_op | source)
XLA Modules:
  0.0 244.1 jit_solution(13199235688223487252)
XLA Ops:
  11.1 16.1 %all_to_all.10 = bf16[8,64,384]{2,1,0:T(8,128)(2,1)S(1)} all-to-all(bf16[8,64,384]{2,1,0:T(8,128)(2,1)S(1)} %pad_maximum_fusion.1), channel_id=1, replica_groups=mesh['y'=4,'xhi'=2,'core'=2,'xlo'=2,'z'=8] {'y','xhi'}, dimensions={0} | all-to-all | bytes 786432 | tf_op jit(solution)/shard_map/all_to_all | solution.py:56
  28.1 2.1 pad_maximum_fusion
  30.7 79.1 %all-gather.2.cloned.1.call-done = bf16[2,256,6144]{2,1,0:T(8,128)(2,1)} async-done(((bf16[2,256,384]{2,1,0:T(8,128)(2,1)}), bf16[2,256,6144]{2,1,0:T(8,128)(2,1)}) %all-gather.2.cloned.1.call-update) | async-done | bytes 6291472 | tf_op jit(solution)/shard_map/all_gather | solution.py:59
  109.8 4.3 %fusion.14 = f32[256,256]{0,1:T(8,128)S(1)} fusion(bf16[2,256,6144]{2,1,0:T(8,128)(2,1)} %all-gather.2.cloned.1.call-done, bf16[6144,128]{1,0:T(8,128)(2,1)} %bitcast.78, bf16[6144,128]{1,0:T(8,128)(2,1)} %bitcast.81), kind=kOutput, calls=%fused_computation.25 | convolution fusion | flops 811597824 | bytes 6553600 | tf_op jit(solution)/shard_map/dot_general | solution.py:69
  114.4 2.7 %multiply_convert_fusion.4 = (bf16[256,128]{0,1:T(8,128)(2,1)S(1)}, bf16[256,128]{0,1:T(8,128)(2,1)S(1)}, bf16[256,128]{0,1:T(8,128)(2,1)S(1)}) fusion(f32[256,256]{0,1:T(8,128)S(1)} %fusion.14, bf16[1,128,6144]{2,1,0:T(8,128)(2,1)} %param.12, bf16[2,256,6144]{2,1,0:T(8,128)(2,1)S(1)} %copy-done.1), kind=kOutput, calls=%fused_computation.46 | convolution fusion | flops 403144704 | bytes 5177344 | tf_op jit(solution)/shard_map/rd,hd->rh/dot_general | solution.py:82
  117.2 1.0 convolution_convert_fusion.2
  118.2 2.4 fusion
  120.7 1.4 fusion.13
  122.1 2.6 %multiply_convert_fusion.1 = (bf16[256,128]{0,1:T(8,128)(2,1)S(1)}, bf16[256,128]{0,1:T(8,128)(2,1)S(1)}, bf16[256,128]{0,1:T(8,128)(2,1)S(1)}) fusion(f32[256,256]{0,1:T(8,128)S(1)} %fusion.13, bf16[128,6144]{1,0:T(8,128)(2,1)} %collective-permute-done.1, bf16[2,256,6144]{2,1,0:T(8,128)(2,1)S(1)} %copy-done.1), kind=kOutput, calls=%fused_computation.41 | convolution fusion | flops 403144704 | bytes 5177344 | tf_op jit(solution)/shard_map/rd,hd->rh/dot_general | solution.py:82
  124.7 2.5 %fusion.1 = bf16[6144,256]{1,0:T(8,128)(2,1)S(1)} fusion(bf16[256,128]{0,1:T(8,128)(2,1)S(1)} %get-tuple-element.13, bf16[128,6144]{1,0:T(8,128)(2,1)} %collective-permute-done.1), kind=kOutput, calls=%fused_computation.6 | convolution fusion | flops 404226048 | bytes 4784128 | tf_op jit(solution)/shard_map/hd,rh->dr/dot_general | solution.py:75
  127.2 1.0 convolution_convert_fusion
  128.2 3.9 %add_convert_fusion = bf16[6144,512]{1,0:T(8,128)(2,1)} fusion(bf16[6144,256]{1,0:T(8,128)(2,1)S(1)} %convolution_convert_fusion.2, bf16[6144,256]{1,0:T(8,128)(2,1)S(1)} %fusion, bf16[6144,256]{1,0:T(8,128)(2,1)S(1)} %convolution_convert_fusion, bf16[6144,256]{1,0:T(8,128)(2,1)S(1)} %fusion.1), kind=kLoop, calls=%fused_computation | loop fusion | flops 31457280 | bytes 18874368 | tf_op jit(solution)/shard_map/convert_element_type | solution.py:105
  133.0 3.1 %fusion.11 = f32[6144,128]{1,0:T(8,128)S(1)} fusion(bf16[256,128]{0,1:T(8,128)(2,1)S(1)} %copy-done.9, bf16[2,256,6144]{2,1,0:T(8,128)(2,1)} %all-gather.2.cloned.1.call-done), kind=kOutput, calls=%fused_computation.22 | convolution fusion | flops 402653184 | bytes 6356992 | tf_op jit(solution)/shard_map/rd,rh->dh/dot_general | solution.py:114
  136.2 1.0 fusion.12
  138.0 2.2 fusion.8
  140.4 1.4 collective-permute-done.3
  141.8 2.2 fusion.6
  144.0 2.2 collective-permute-done.2
  146.3 2.3 fusion.7
  148.5 68.6 %reduce-scatter.2.cloned.1.call-done = bf16[384,512]{1,0:T(8,128)(2,1)} async-done(((bf16[6144,512]{1,0:T(8,128)(2,1)}), bf16[384,512]{1,0:T(8,128)(2,1)}) %reduce-scatter.2.cloned.1.call-update) | async-done | bytes 393232 | tf_op jit(solution)/shard_map/reduce_scatter | solution.py:106
  217.2 1.0 slice_bitcast_fusion.13
  219.4 6.5 %all-to-all-start.1 = ((bf16[8,64,384]{2,1,0:T(8,128)(2,1)}), bf16[8,64,384]{2,1,0:T(8,128)(2,1)S(1)}, u32[]{:S(2)}, u32[]{:S(2)}) async-start(bf16[8,64,384]{2,1,0:T(8,128)(2,1)} %pad_maximum_fusion.2), calls=%async_computation.2 | async-start | bytes 786432 | tf_op jit(solution)/shard_map/all_to_all | solution.py:131
  225.8 4.6 %fusion.5 = bf16[1,128,6144]{2,1,0:T(8,128)(2,1)} fusion(f32[128,6144]{1,0:T(8,128)} %collective-permute-done.4, bf16[256,128]{0,1:T(8,128)(2,1)S(1)} %get-tuple-element.14, bf16[2,256,6144]{2,1,0:T(8,128)(2,1)} %all-gather.2.cloned.1.call-done), kind=kOutput, calls=%fused_computation.13 | convolution fusion | flops 404226048 | bytes 7929856 | tf_op jit(solution)/shard_map/rh,rd->hd/dot_general | solution.py:115
  230.5 4.9 %all-to-all-done.1 = bf16[8,64,384]{2,1,0:T(8,128)(2,1)S(1)} async-done(((bf16[8,64,384]{2,1,0:T(8,128)(2,1)}), bf16[8,64,384]{2,1,0:T(8,128)(2,1)S(1)}, u32[]{:S(2)}, u32[]{:S(2)}) %all-to-all-start.1) | async-done | bytes 393248 | tf_op jit(solution)/shard_map/all_to_all | solution.py:131
  (68 shorter events, 10.5 us)
Async XLA Ops:
  7.2 2.6 %copy-start = (bf16[48,384]{1,0:T(8,128)(2,1)S(1)}, bf16[48,384]{1,0:T(8,128)(2,1)}, u32[]{:S(2)}) copy-start(bf16[48,384]{1,0:T(8,128)(2,1)} %param.13) | copy-start | bytes 110596
  7.2 20.9 %copy-start.4 = (bf16[1,6144,128]{2,1,0:T(8,128)(2,1)S(1)}, bf16[1,6144,128]{2,1,0:T(8,128)(2,1)}, u32[]{:S(2)}) copy-start(bf16[1,6144,128]{2,1,0:T(8,128)(2,1)} %param.10) | copy-start | bytes 4718596
  7.2 20.9 %copy-start.2 = (bf16[1,6144,128]{2,1,0:T(8,128)(2,1)S(1)}, bf16[1,6144,128]{2,1,0:T(8,128)(2,1)}, u32[]{:S(2)}) copy-start(bf16[1,6144,128]{2,1,0:T(8,128)(2,1)} %param.11) | copy-start | bytes 4718596
  7.2 102.6 %all-gather.2.cloned.1.call-start = ((), (), s32[]{:S(2)}) async-start(), calls=%async_computation.3 | async-start | bytes 6684672 | tf_op jit(solution)/shard_map/all_gather | solution.py:59
  28.0 189.1 %reduce-scatter.2.cloned.1.call-start = ((), (), s32[]{:S(2)}) async-start(), calls=%async_computation.4 | async-start | bytes 6684672 | tf_op jit(solution)/shard_map/reduce_scatter | solution.py:106
  30.2 90.5 %collective-permute-start = (bf16[6144,256]{1,0:T(8,128)(2,1)}, bf16[6144,256]{1,0:T(8,128)(2,1)S(1)}, u32[]{:S(2)}, u32[]{:S(2)}) collective-permute-start(bf16[6144,256]{1,0:T(8,128)(2,1)} %pad_maximum_fusion), channel_id=1, source_target_pairs={{0,16},{16,0},{1,17},{17,1},{2,18},{18,2},{3,19},{19,3},{4,20},{20... | collective-permute-start | bytes 9437192 | tf_op jit(solution)/shard_map/ppermute | solution.py:66
  30.2 91.9 %collective-permute-start.1 = (bf16[128,6144]{1,0:T(8,128)(2,1)}, bf16[128,6144]{1,0:T(8,128)(2,1)}, u32[]{:S(2)}, u32[]{:S(2)}) collective-permute-start(bf16[128,6144]{1,0:T(8,128)(2,1)} %bitcast.10), channel_id=1, source_target_pairs={{0,16},{16,0},{1,17},{17,1},{2,18},{18,2},{3,19},{19,3},{4,20},{20... | collective-permute-start | bytes 4718600 | tf_op jit(solution)/shard_map/ppermute | solution.py:66
  109.8 4.7 %copy-start.1 = (bf16[2,256,6144]{2,1,0:T(8,128)(2,1)S(1)}, bf16[2,256,6144]{2,1,0:T(8,128)(2,1)}, u32[]{:S(2)}) copy-start(bf16[2,256,6144]{2,1,0:T(8,128)(2,1)} %all-gather.2.cloned.1.call-done) | copy-start | bytes 18874372
  114.4 2.8 %copy-start.3 = (bf16[1,6144,128]{2,1,0:T(8,128)(2,1)S(1)}, bf16[1,6144,128]{2,1,0:T(8,128)(2,1)}, u32[]{:S(2)}) copy-start(bf16[1,6144,128]{2,1,0:T(8,128)(2,1)} %param.11) | copy-start | bytes 4718596
  114.4 2.8 %copy-start.5 = (bf16[1,6144,128]{2,1,0:T(8,128)(2,1)S(1)}, bf16[1,6144,128]{2,1,0:T(8,128)(2,1)}, u32[]{:S(2)}) copy-start(bf16[1,6144,128]{2,1,0:T(8,128)(2,1)} %param.10) | copy-start | bytes 4718596
  117.2 1.0 copy-start.10
  117.2 1.0 copy-start.12
  124.7 2.5 %copy-start.6 = (bf16[256,128]{0,1:T(8,128)(2,1)}, bf16[256,128]{0,1:T(8,128)(2,1)S(1)}, u32[]{:S(2)}) copy-start(bf16[256,128]{0,1:T(8,128)(2,1)S(1)} %get-tuple-element.9) | copy-start | bytes 196612
  124.7 2.5 %copy-start.8 = (bf16[256,128]{0,1:T(8,128)(2,1)}, bf16[256,128]{0,1:T(8,128)(2,1)S(1)}, u32[]{:S(2)}) copy-start(bf16[256,128]{0,1:T(8,128)(2,1)S(1)} %get-tuple-element.10) | copy-start | bytes 196612
  132.1 0.8 copy-start.9
  132.1 4.0 %slice-start = ((s8[6291456]{0:T(1024)(128)(4,1)}), s8[2097152]{0:T(1024)(128)(4,1)S(1)}, s32[]{:S(2)}) async-start(s8[6291456]{0:T(1024)(128)(4,1)} %bitcast.74), calls=%async_computation.5 | async-start | bytes 4194304
  132.9 3.3 %slice-start.1 = ((s8[6291456]{0:T(1024)(128)(4,1)}), s8[4194304]{0:T(1024)(128)(4,1)S(1)}, s32[]{:S(2)}) async-start(s8[6291456]{0:T(1024)(128)(4,1)} %bitcast.74), calls=%async_computation.6 | async-start | bytes 8388608
  133.0 3.3 %copy-start.7 = (bf16[256,128]{0,1:T(8,128)(2,1)S(1)}, bf16[256,128]{0,1:T(8,128)(2,1)}, u32[]{:S(2)}) copy-start(bf16[256,128]{0,1:T(8,128)(2,1)} %copy-done.6) | copy-start | bytes 196612
  136.0 5.7 %collective-permute-start.3 = (f32[6144,128]{1,0:T(8,128)S(1)}, f32[6144,128]{1,0:T(8,128)S(1)}, u32[]{:S(2)}, u32[]{:S(2)}) collective-permute-start(f32[6144,128]{1,0:T(8,128)S(1)} %fusion.11), channel_id=1, source_target_pairs={{0,16},{16,0},{1,17},{17,1},{2,18},{18,2},{3,19},{19,3},{4,20},{20... | collective-permute-start | bytes 9437192 | tf_op jit(solution)/shard_map/ppermute | solution.py:119
  137.3 4.5 %copy-start.13 = (bf16[256,128]{0,1:T(8,128)(2,1)S(1)}, bf16[256,128]{0,1:T(8,128)(2,1)}, u32[]{:S(2)}) copy-start(bf16[256,128]{0,1:T(8,128)(2,1)} %copy-done.12) | copy-start | bytes 196612
  137.3 9.0 %collective-permute-start.2 = (f32[6144,128]{1,0:T(8,128)S(1)}, f32[6144,128]{1,0:T(8,128)S(1)}, u32[]{:S(2)}, u32[]{:S(2)}) collective-permute-start(f32[6144,128]{1,0:T(8,128)S(1)} %fusion.12), channel_id=1, source_target_pairs={{0,16},{16,0},{1,17},{17,1},{2,18},{18,2},{3,19},{19,3},{4,20},{20... | collective-permute-start | bytes 9437192 | tf_op jit(solution)/shard_map/ppermute | solution.py:119
  140.2 6.0 %copy-start.11 = (bf16[256,128]{0,1:T(8,128)(2,1)S(1)}, bf16[256,128]{0,1:T(8,128)(2,1)}, u32[]{:S(2)}) copy-start(bf16[256,128]{0,1:T(8,128)(2,1)} %copy-done.10) | copy-start | bytes 196612
  140.2 85.6 %collective-permute-start.4 = (f32[128,6144]{1,0:T(8,128)}, f32[128,6144]{1,0:T(8,128)}, u32[]{:S(2)}, u32[]{:S(2)}) collective-permute-start(f32[128,6144]{1,0:T(8,128)} %fusion.8), channel_id=1, source_target_pairs={{0,16},{16,0},{1,17},{17,1},{2,18},{18,2},{3,19},{19,3},{4,20},{20... | collective-permute-start | bytes 9437192 | tf_op jit(solution)/shard_map/ppermute | solution.py:119
  219.4 16.0 %all-to-all-start.1 = ((bf16[8,64,384]{2,1,0:T(8,128)(2,1)}), bf16[8,64,384]{2,1,0:T(8,128)(2,1)S(1)}, u32[]{:S(2)}, u32[]{:S(2)}) async-start(bf16[8,64,384]{2,1,0:T(8,128)(2,1)} %pad_maximum_fusion.2), calls=%async_computation.2 | async-start | bytes 786432 | tf_op jit(solution)/shard_map/all_to_all | solution.py:131
Sparse Core Ops, SparseCore 0:
  28.2 81.5 all-gather.1
  132.3 84.8 reduce-scatter.1

commit v8 on v7

--- a/solution.py
+++ b/solution.py
@@ -65,8 +65,7 @@
     gu_local = jnp.concatenate([gate_local, up_local], axis=1)
     gu_other, down_other = lax.ppermute((gu_local, down_local), "core", pair)
 
-    def forward(rows, gu_w, down_w):
-        pre = jnp.dot(rows, gu_w, preferred_element_type=jnp.float32)
+    def forward(pre, gu_w, down_w):
         width = pre.shape[1] // 2
         gate_pre, up_pre = pre[:, :width], pre[:, width:]
         sigmoid_gate = jax.nn.sigmoid(gate_pre)
@@ -78,10 +77,7 @@
         out_t = with_layout_constraint(out_t, Layout(major_to_minor=(0, 1)))
         return gate_pre, up_pre, sigmoid_gate, activated, hidden, out_t
 
-    def backward(grads, gate_pre, up_pre, sigmoid_gate, activated, gu_w, down_w):
-        hidden_grad = jnp.einsum(
-            "rd,hd->rh", grads, down_w, preferred_element_type=jnp.float32
-        )
+    def backward(hidden_grad, gate_pre, up_pre, sigmoid_gate, activated, gu_w, down_w):
         gate_grad = (
             hidden_grad * up_pre * sigmoid_gate * (1.0 + gate_pre * (1.0 - sigmoid_gate))
         ).astype(jnp.bfloat16)
@@ -96,10 +92,20 @@
     rows, grads = mine_full[0], mine_full[1]
     own_w = (gu_local, down_local)
     other_w = (gu_other, down_other)
-    f_own = forward(rows, *own_w)
-    f_other = forward(rows, *other_w)
-    b_own = backward(grads, *f_own[:4], *own_w)
-    b_other = backward(grads, *f_other[:4], *other_w)
+    width = gu_local.shape[1]
+    pre_both = jnp.dot(
+        rows, jnp.concatenate([gu_local, gu_other], axis=1), preferred_element_type=jnp.float32
+    )
+    hgrad_both = jnp.einsum(
+        "rd,hd->rh",
+        grads,
+        jnp.concatenate([down_local, down_other], axis=0),
+        preferred_element_type=jnp.float32,
+    )
+    f_own = forward(pre_both[:, :width], *own_w)
+    f_other = forward(pre_both[:, width:], *other_w)
+    b_own = backward(hgrad_both[:, : width // 2], *f_own[:4], *own_w)
+    b_other = backward(hgrad_both[:, width // 2 :], *f_other[:4], *other_w)
     own = jnp.concatenate([f_own[5], b_own[2]], axis=1)
     other = jnp.concatenate([f_other[5], b_other[2]], axis=1)
     summed = (own.astype(jnp.float32) + other.astype(jnp.float32)).astype(jnp.bfloat16)

time: 244 us -> 241 us (0.988)
  matrix products: 36.5 us -> 33.3 us
    ppermute x2, waiting for transfers between devices: 0.01 us -> 5.15 us  [per_device(): gu_other, down_other = lax.ppermute((gu_local, down_local), 'core', pair)]
    all_gather x1, waiting for transfers between devices: 79.1 us -> 75.5 us  [per_device(): mine_full = lax.all_gather(mine, TN, axis=2, tiled=True)]
    dot_general x4 -> x2, matrix products: 11 us -> 7.69 us  [the longest x1 4.8 us: per_device(): jnp.dot(rows, jnp.concatenate([gu_local, gu_other], axis=1), preferred_el...]
  transfers between devices with their start and end apart: 8 -> 8, of which waited for: 5 -> 6; matrix products, arithmetic and copies ran while one was open for 13% -> 9% of each run, Pallas kernels for 0% -> 0%
where the time goes in v8:
time: 241 us; the launch traced here: 240 us
  waiting for transfers between devices  158 us (66%)
  matrix products  33.3 us (14%)
  blocking collectives  16.1 us (7%)
  between operations  14.4 us (6%)
  other arithmetic  7.59 us (3%)
  starting transfers between devices  7.13 us (3%)
  local copies, waits for them, and re-layouts  3.4 us (1%)
    all_gather x1, waiting for transfers between devices, per_device(): mine_full = lax.all_gather(mine, TN, axis=2, tiled=True)  75.5 us
    reduce_scatter x1, waiting for transfers between devices, per_device(): scattered = lax.psum_scatter(summed, TN, scatter_dimension=0, tiled=True)  69 us
    all_to_all x1, blocking collectives, per_device(): recv = lax.all_to_all(send, SRC, split_axis=0, concat_axis=0, tiled=True)  16.1 us
    dot_general x2, matrix products, weight_grads(): jnp.einsum('rh,rd->hd', f[4], grads, preferred_element_type=jnp.float32)  6.87 us
    all_to_all x1, starting transfers between devices, per_device(): lax.all_to_all(done, SRC, split_axis=0, concat_axis=0, tiled=True)  5.59 us
    dot_general x2, matrix products, weight_grads(): jnp.einsum('rd,rh->dh', rows, b[1], preferred_element_type=jnp.float32)  5.32 us
    ppermute x2, waiting for transfers between devices, per_device(): gu_other, down_other = lax.ppermute((gu_local, down_local), 'core', pair)  5.15 us
    dot_general x2, matrix products, forward(): jnp.einsum('hd,rh->dr', down_w, hidden, preferred_element_type=jnp.float32)  5.07 us
  transfers between devices with their start and end apart: 8, of which 6 were waited for; matrix products, arithmetic and copies ran while one was open for 9% of the time, Pallas kernels for 0%

profile of v8, /device:TPU:2, one launch (start us, length us, event | category | flops | bytes accessed | tf_op | source)
XLA Modules:
  0.0 240.3 jit_solution(1196696518437505472)
XLA Ops:
  10.1 1.0 convolution_convert_fusion.4
  11.1 16.1 %all_to_all.10 = bf16[8,64,384]{2,1,0:T(8,128)(2,1)S(1)} all-to-all(bf16[8,64,384]{2,1,0:T(8,128)(2,1)S(1)} %pad_maximum_fusion.1), channel_id=1, replica_groups=mesh['y'=4,'xhi'=2,'core'=2,'xlo'=2,'z'=8] {'y','xhi'}, dimensions={0} | all-to-all | bytes 786432 | tf_op jit(solution)/shard_map/all_to_all | solution.py:56
  29.1 5.1 %collective-permute-done = bf16[6144,256]{1,0:T(8,128)(2,1)S(1)} collective-permute-done((bf16[6144,256]{1,0:T(8,128)(2,1)S(1)}, bf16[6144,256]{1,0:T(8,128)(2,1)S(1)}, u32[]{:S(2)}, u32[]{:S(2)}) %collective-permute-start) | collective-permute-done | bytes 3145760 | tf_op jit(solution)/shard_map/ppermute | solution.py:66
  34.2 75.5 %all-gather.2.cloned.1.call-done = bf16[2,256,6144]{2,1,0:T(8,128)(2,1)} async-done(((bf16[2,256,384]{2,1,0:T(8,128)(2,1)}), bf16[2,256,6144]{2,1,0:T(8,128)(2,1)}) %all-gather.2.cloned.1.call-update) | async-done | bytes 6291472 | tf_op jit(solution)/shard_map/all_gather | solution.py:59
  109.8 4.8 %fusion.8 = f32[256,512]{1,0:T(8,128)S(1)} fusion(bf16[6144,256]{1,0:T(8,128)(2,1)S(1)} %collective-permute-done, bf16[6144,128]{1,0:T(8,128)(2,1)} %bitcast.66, bf16[6144,128]{1,0:T(8,128)(2,1)} %bitcast.69, bf16[2,256,6144]{2,1,0:T(8,128)(2,1)} %all-gather.2.cloned.1.call-done), kind=kOutput, calls=%fused_computation.16 | convolution fusion | flops 1629487104 | bytes 9961472 | tf_op jit(solution)/shard_map/dot_general | solution.py:96
  114.6 2.9 %fusion.14 = f32[256,256]{1,0:T(8,128)S(1)} fusion(bf16[128,6144]{1,0:T(8,128)(2,1)} %collective-permute-done.1, bf16[128,6144]{1,0:T(8,128)(2,1)} %bitcast.10, bf16[2,256,6144]{2,1,0:T(8,128)(2,1)S(1)} %copy-done.2), kind=kOutput, calls=%fused_computation.25 | convolution fusion | flops 811597824 | bytes 6553600 | tf_op jit(solution)/shard_map/rd,hd->rh/dot_general | solution.py:99
  117.8 2.6 %fusion = bf16[6144,256]{1,0:T(8,128)(2,1)S(1)} fusion(bf16[256,128]{1,0:T(8,128)(2,1)S(1)} %get-tuple-element.10, bf16[1,128,6144]{2,1,0:T(8,128)(2,1)} %param.12), kind=kOutput, calls=%fused_computation.5 | convolution fusion | flops 404226048 | bytes 4784128 | tf_op jit(solution)/shard_map/hd,rh->dr/dot_general | solution.py:74
  120.4 1.0 convolution_convert_fusion.2
  121.5 2.4 %fusion.1 = bf16[6144,256]{1,0:T(8,128)(2,1)S(1)} fusion(bf16[256,128]{1,0:T(8,128)(2,1)S(1)} %get-tuple-element.9, bf16[128,6144]{1,0:T(8,128)(2,1)} %collective-permute-done.1), kind=kOutput, calls=%fused_computation.6 | convolution fusion | flops 404226048 | bytes 4784128 | tf_op jit(solution)/shard_map/hd,rh->dr/dot_general | solution.py:74
  123.9 1.0 convolution_convert_fusion
  124.9 3.9 %add_convert_fusion = bf16[6144,512]{1,0:T(8,128)(2,1)} fusion(bf16[6144,256]{1,0:T(8,128)(2,1)S(1)} %convolution_convert_fusion.2, bf16[6144,256]{1,0:T(8,128)(2,1)S(1)} %fusion, bf16[6144,256]{1,0:T(8,128)(2,1)S(1)} %convolution_convert_fusion, bf16[6144,256]{1,0:T(8,128)(2,1)S(1)} %fusion.1), kind=kLoop, calls=%fused_computation | loop fusion | flops 31457280 | bytes 18874368 | tf_op jit(solution)/shard_map/convert_element_type | solution.py:111
  129.7 3.1 %fusion.19 = f32[6144,128]{1,0:T(8,128)S(1)} fusion(bf16[256,128]{1,0:T(8,128)(2,1)S(1)} %copy-done.8, bf16[2,256,6144]{2,1,0:T(8,128)(2,1)} %all-gather.2.cloned.1.call-done), kind=kOutput, calls=%fused_computation.30 | convolution fusion | flops 402653184 | bytes 6356992 | tf_op jit(solution)/shard_map/rd,rh->dh/dot_general | solution.py:120
  133.0 1.0 fusion.20
  134.7 2.3 fusion.18
  137.0 1.5 collective-permute-done.3
  138.5 2.2 fusion.6
  140.7 2.2 collective-permute-done.2
  143.0 2.2 fusion.7
  145.3 69.0 %reduce-scatter.2.cloned.1.call-done = bf16[384,512]{1,0:T(8,128)(2,1)} async-done(((bf16[6144,512]{1,0:T(8,128)(2,1)}), bf16[384,512]{1,0:T(8,128)(2,1)}) %reduce-scatter.2.cloned.1.call-update) | async-done | bytes 393232 | tf_op jit(solution)/shard_map/reduce_scatter | solution.py:112
  214.3 1.0 slice_bitcast_fusion.11
  216.5 5.6 %all-to-all-start.1 = ((bf16[8,64,384]{2,1,0:T(8,128)(2,1)}), bf16[8,64,384]{2,1,0:T(8,128)(2,1)S(1)}, u32[]{:S(2)}, u32[]{:S(2)}) async-start(bf16[8,64,384]{2,1,0:T(8,128)(2,1)} %pad_maximum_fusion.2), calls=%async_computation.2 | async-start | bytes 786432 | tf_op jit(solution)/shard_map/all_to_all | solution.py:137
  222.1 4.6 %fusion.5 = bf16[1,128,6144]{2,1,0:T(8,128)(2,1)} fusion(f32[128,6144]{1,0:T(8,128)} %collective-permute-done.4, bf16[256,128]{1,0:T(8,128)(2,1)S(1)} %get-tuple-element.10, bf16[2,256,6144]{2,1,0:T(8,128)(2,1)} %all-gather.2.cloned.1.call-done), kind=kOutput, calls=%fused_computation.13 | convolution fusion | flops 404226048 | bytes 7929856 | tf_op jit(solution)/shard_map/rh,rd->hd/dot_general | solution.py:121
  226.7 4.8 %all-to-all-done.1 = bf16[8,64,384]{2,1,0:T(8,128)(2,1)S(1)} async-done(((bf16[8,64,384]{2,1,0:T(8,128)(2,1)}), bf16[8,64,384]{2,1,0:T(8,128)(2,1)S(1)}, u32[]{:S(2)}, u32[]{:S(2)}) %all-to-all-start.1) | async-done | bytes 393248 | tf_op jit(solution)/shard_map/all_to_all | solution.py:137
  231.6 0.9 convolution_convert_fusion.7
  (69 shorter events, 8.8 us)
Async XLA Ops:
  7.2 2.6 %copy-start = (bf16[48,384]{1,0:T(8,128)(2,1)S(1)}, bf16[48,384]{1,0:T(8,128)(2,1)}, u32[]{:S(2)}) copy-start(bf16[48,384]{1,0:T(8,128)(2,1)} %param.13) | copy-start | bytes 110596
  7.2 20.9 %copy-start.5 = (bf16[1,6144,128]{2,1,0:T(8,128)(2,1)S(1)}, bf16[1,6144,128]{2,1,0:T(8,128)(2,1)}, u32[]{:S(2)}) copy-start(bf16[1,6144,128]{2,1,0:T(8,128)(2,1)} %param.10) | copy-start | bytes 4718596
  7.2 20.9 %copy-start.3 = (bf16[1,6144,128]{2,1,0:T(8,128)(2,1)S(1)}, bf16[1,6144,128]{2,1,0:T(8,128)(2,1)}, u32[]{:S(2)}) copy-start(bf16[1,6144,128]{2,1,0:T(8,128)(2,1)} %param.11) | copy-start | bytes 4718596
  7.2 102.6 %all-gather.2.cloned.1.call-start = ((), (), s32[]{:S(2)}) async-start(), calls=%async_computation.3 | async-start | bytes 6684672 | tf_op jit(solution)/shard_map/all_gather | solution.py:59
  9.7 1.3 copy-start.9
  28.1 186.2 %reduce-scatter.2.cloned.1.call-start = ((), (), s32[]{:S(2)}) async-start(), calls=%async_computation.4 | async-start | bytes 6684672 | tf_op jit(solution)/shard_map/reduce_scatter | solution.py:112
  28.5 5.7 %collective-permute-start = (bf16[6144,256]{1,0:T(8,128)(2,1)S(1)}, bf16[6144,256]{1,0:T(8,128)(2,1)S(1)}, u32[]{:S(2)}, u32[]{:S(2)}) collective-permute-start(bf16[6144,256]{1,0:T(8,128)(2,1)S(1)} %pad_maximum_fusion), channel_id=1, source_target_pairs={{0,16},{16,0},{1,17},{17,1},{2,18},{18,2},{3,19},{19,3},{4,20},{20... | collective-permute-start | bytes 9437192 | tf_op jit(solution)/shard_map/ppermute | solution.py:66
  28.6 86.0 %collective-permute-start.1 = (bf16[128,6144]{1,0:T(8,128)(2,1)}, bf16[128,6144]{1,0:T(8,128)(2,1)}, u32[]{:S(2)}, u32[]{:S(2)}) collective-permute-start(bf16[128,6144]{1,0:T(8,128)(2,1)} %bitcast.10), channel_id=1, source_target_pairs={{0,16},{16,0},{1,17},{17,1},{2,18},{18,2},{3,19},{19,3},{4,20},{20... | collective-permute-start | bytes 4718600 | tf_op jit(solution)/shard_map/ppermute | solution.py:66
  109.8 4.8 %copy-start.2 = (bf16[2,256,6144]{2,1,0:T(8,128)(2,1)S(1)}, bf16[2,256,6144]{2,1,0:T(8,128)(2,1)}, u32[]{:S(2)}) copy-start(bf16[2,256,6144]{2,1,0:T(8,128)(2,1)} %all-gather.2.cloned.1.call-done) | copy-start | bytes 18874372
  117.5 2.9 %copy-start.4 = (bf16[1,6144,128]{2,1,0:T(8,128)(2,1)S(1)}, bf16[1,6144,128]{2,1,0:T(8,128)(2,1)}, u32[]{:S(2)}) copy-start(bf16[1,6144,128]{2,1,0:T(8,128)(2,1)} %param.11) | copy-start | bytes 4718596
  117.5 2.9 %copy-start.6 = (bf16[1,6144,128]{2,1,0:T(8,128)(2,1)S(1)}, bf16[1,6144,128]{2,1,0:T(8,128)(2,1)}, u32[]{:S(2)}) copy-start(bf16[1,6144,128]{2,1,0:T(8,128)(2,1)} %param.10) | copy-start | bytes 4718596
  117.7 3.7 %copy-start.11 = (bf16[256,128]{1,0:T(8,128)(2,1)}, bf16[256,128]{1,0:T(8,128)(2,1)S(1)}, u32[]{:S(2)}) copy-start(bf16[256,128]{1,0:T(8,128)(2,1)S(1)} %get-tuple-element.8) | copy-start | bytes 196612
  117.7 3.7 %copy-start.13 = (bf16[256,128]{1,0:T(8,128)(2,1)}, bf16[256,128]{1,0:T(8,128)(2,1)S(1)}, u32[]{:S(2)}) copy-start(bf16[256,128]{1,0:T(8,128)(2,1)S(1)} %get-tuple-element.6) | copy-start | bytes 196612
  117.8 6.2 %copy-start.7 = (bf16[256,128]{1,0:T(8,128)(2,1)}, bf16[256,128]{1,0:T(8,128)(2,1)S(1)}, u32[]{:S(2)}) copy-start(bf16[256,128]{1,0:T(8,128)(2,1)S(1)} %get-tuple-element.7) | copy-start | bytes 196612
  128.8 4.0 %slice-start = ((s8[6291456]{0:T(1024)(128)(4,1)}), s8[2097152]{0:T(1024)(128)(4,1)S(1)}, s32[]{:S(2)}) async-start(s8[6291456]{0:T(1024)(128)(4,1)} %bitcast.62), calls=%async_computation.5 | async-start | bytes 4194304
  129.7 3.3 %slice-start.1 = ((s8[6291456]{0:T(1024)(128)(4,1)}), s8[4194304]{0:T(1024)(128)(4,1)S(1)}, s32[]{:S(2)}) async-start(s8[6291456]{0:T(1024)(128)(4,1)} %bitcast.62), calls=%async_computation.6 | async-start | bytes 8388608
  132.8 5.7 %collective-permute-start.3 = (f32[6144,128]{1,0:T(8,128)S(1)}, f32[6144,128]{1,0:T(8,128)S(1)}, u32[]{:S(2)}, u32[]{:S(2)}) collective-permute-start(f32[6144,128]{1,0:T(8,128)S(1)} %fusion.19), channel_id=1, source_target_pairs={{0,16},{16,0},{1,17},{17,1},{2,18},{18,2},{3,19},{19,3},{4,20},{20... | collective-permute-start | bytes 9437192 | tf_op jit(solution)/shard_map/ppermute | solution.py:125
  134.0 4.5 %copy-start.14 = (bf16[256,128]{1,0:T(8,128)(2,1)S(1)}, bf16[256,128]{1,0:T(8,128)(2,1)}, u32[]{:S(2)}) copy-start(bf16[256,128]{1,0:T(8,128)(2,1)} %copy-done.13) | copy-start | bytes 196612
  134.0 9.0 %collective-permute-start.2 = (f32[6144,128]{1,0:T(8,128)S(1)}, f32[6144,128]{1,0:T(8,128)S(1)}, u32[]{:S(2)}, u32[]{:S(2)}) collective-permute-start(f32[6144,128]{1,0:T(8,128)S(1)} %fusion.20), channel_id=1, source_target_pairs={{0,16},{16,0},{1,17},{17,1},{2,18},{18,2},{3,19},{19,3},{4,20},{20... | collective-permute-start | bytes 9437192 | tf_op jit(solution)/shard_map/ppermute | solution.py:125
  136.9 6.1 %copy-start.12 = (bf16[256,128]{1,0:T(8,128)(2,1)S(1)}, bf16[256,128]{1,0:T(8,128)(2,1)}, u32[]{:S(2)}) copy-start(bf16[256,128]{1,0:T(8,128)(2,1)} %copy-done.11) | copy-start | bytes 196612
  136.9 85.2 %collective-permute-start.4 = (f32[128,6144]{1,0:T(8,128)}, f32[128,6144]{1,0:T(8,128)}, u32[]{:S(2)}, u32[]{:S(2)}) collective-permute-start(f32[128,6144]{1,0:T(8,128)} %fusion.18), channel_id=1, source_target_pairs={{0,16},{16,0},{1,17},{17,1},{2,18},{18,2},{3,19},{19,3},{4,20},{20... | collective-permute-start | bytes 9437192 | tf_op jit(solution)/shard_map/ppermute | solution.py:125
  216.5 15.1 %all-to-all-start.1 = ((bf16[8,64,384]{2,1,0:T(8,128)(2,1)}), bf16[8,64,384]{2,1,0:T(8,128)(2,1)S(1)}, u32[]{:S(2)}, u32[]{:S(2)}) async-start(bf16[8,64,384]{2,1,0:T(8,128)(2,1)} %pad_maximum_fusion.2), calls=%async_computation.2 | async-start | bytes 786432 | tf_op jit(solution)/shard_map/all_to_all | solution.py:137
  222.1 10.5 %copy-start.10 = (f32[48,4,32]{0,2,1:T(8,128)S(1)}, f32[48,4,32]{0,2,1:T(8,128)}, u32[]{:S(2)}) copy-start(f32[48,4,32]{0,2,1:T(8,128)} %copy-done.9) | copy-start | bytes 73732
  222.1 11.4 %copy-start.1 = (bf16[48,384]{1,0:T(8,128)(2,1)S(1)}, bf16[48,384]{1,0:T(8,128)(2,1)}, u32[]{:S(2)}) copy-start(bf16[48,384]{1,0:T(8,128)(2,1)} %param.13) | copy-start | bytes 110596
  (1 other events, 0.8 us)
Sparse Core Ops, SparseCore 0:
  28.2 81.5 all-gather.1
  129.0 85.2 reduce-scatter.1
